TPU v7x, 32 devices: a whole 2x2x4 slice. The times are simulated.
32 devices in a mesh: pair: 8 (over z, core), orb: 4 (over y, x).
Axes of the slice: x: 2, y: 2, z: 4, core: 2. Of those that a mesh axis runs over, the one named last changes fastest.
Arguments:
- amplitudes: bfloat16 [8, 2, 600, 600], P('pair', None, 'orb'), may hold values from -6 to 6
- factors: bfloat16 [48, 360000], P('orb', 'pair'), may hold values from -0.21875 to 0.21875
- crossed_amplitudes: bfloat16 [8, 64, 600, 600], P('pair', None, 'orb'), may hold values from -6 to 6
- crossed_coupling: bfloat16 [38400, 1200], P('orb', 'pair'), may hold values from -0.03125 to 0.03125
Outputs:
- residual: float32 [8, 600, 2, 600], P('pair', 'orb')
All inputs are finite; a program needn't handle non-finite values.
Results may differ from a plain program's by a relative error of at most 0.0023.
Values may be sent and summed in bfloat16 or wider, within the bound.
No kernel may reach another device: no remote copies, remote signals or barrier semaphores. Data moves between devices by JAX's collectives and lax.ppermute only.
A program may use at most 256 MiB of HBM per device.

v0:
```python
import jax
import jax.numpy as jnp
from jax import lax
from jax.sharding import PartitionSpec as P

NV = 600


def ladder_term(amplitudes, factors, nvirt):
    pair_amps = lax.all_gather(amplitudes, "orb", axis=2, tiled=True)
    factor_rows = lax.all_gather(factors, "pair", axis=1, tiled=True)
    cube = factor_rows.reshape(factor_rows.shape[0], nvirt, nvirt)
    inner = jnp.einsum(
        "qac,jcd->jqad", cube, pair_amps[0], preferred_element_type=jnp.float32
    ).astype(jnp.bfloat16)
    return jnp.einsum("jqad,qbd->ajb", inner, cube, preferred_element_type=jnp.float32)


def crossed_term(crossed_amplitudes, crossed_coupling, nvirt):
    relaid = lax.all_to_all(crossed_amplitudes[0], "orb", split_axis=0, concat_axis=1, tiled=True)
    k_local = relaid.shape[0]
    piece = lax.all_gather(crossed_coupling, "pair", axis=1, tiled=True)
    block = piece.reshape(k_local, nvirt, piece.shape[1])
    product = jnp.einsum("kac,kcn->an", relaid, block, preferred_element_type=jnp.float32)
    return product.reshape(nvirt, product.shape[1] // nvirt, nvirt)


def on_device(amplitudes, factors, crossed_amplitudes, crossed_coupling):
    nvirt = NV
    ladder = ladder_term(amplitudes, factors, nvirt)
    crossed = crossed_term(crossed_amplitudes, crossed_coupling, nvirt)
    total = lax.psum_scatter(ladder, "orb", scatter_dimension=0, tiled=True) + lax.psum_scatter(
        crossed, "orb", scatter_dimension=0, tiled=True
    )
    return total[None]


def solution(mesh):
    return jax.shard_map(
        on_device,
        mesh=mesh,
        in_specs=(
            P("pair", None, "orb", None),
            P("orb", "pair"),
            P("pair", None, "orb", None),
            P("orb", "pair"),
        ),
        out_specs=P("pair", "orb", None, None),
        check_vma=False,
    )
```

profile of v0, /device:TPU:0, one launch (start us, length us, event | category | flops | bytes accessed | tf_op | source)
XLA Modules:
  0.0 646.5 jit_solution(15938430260463364513)
XLA Ops:
  6.5 0.0 all-gather.6.cloned.1.call-start
  6.5 0.7 all-gather.6.cloned.1.call-update
  7.3 0.0 all-gather.8.cloned.1.call-start
  7.3 0.7 all-gather.8.cloned.1.call-update
  8.0 0.0 all-gather.10.cloned.1.call-start
  8.1 0.7 all-gather.10.cloned.1.call-update
  8.7 14.3 %copy.40 = bf16[1,64,150,600]{3,2,1,0:T(8,128)(2,1)} copy(bf16[1,64,150,600]{3,1,2,0:T(8,128)(2,1)} %param.6) | data formatting | bytes 23040000 | tf_op args[2]
  23.1 6.4 all-to-all-start
  29.4 0.3 all-reduce.3.cloned.1.call-start
  29.7 87.7 %all-gather.6.cloned.1.call-done = bf16[1,2,600,600]{3,1,0,2:T(2,128)(2,1)} async-done(((bf16[1,2,150,600]{3,1,0,2:T(2,128)(2,1)}), bf16[1,2,600,600]{3,1,0,2:T(2,128)(2,1)}) %all-gather.6.cloned.1.call-update) | async-done | bytes 1440016 | tf_op jit(solution)/shard_map/all_gather | solution.py:10
  117.4 3.8 copy.19
  121.2 53.8 %all-to-all-done = bf16[64,150,600]{2,1,0:T(8,128)(2,1)} async-done(((bf16[64,150,600]{2,1,0:T(8,128)(2,1)}), bf16[64,150,600]{2,1,0:T(8,128)(2,1)}, u32[]{:S(2)}, u32[]{:S(2)}) %all-to-all-start) | async-done | bytes 11520032 | tf_op jit(solution)/shard_map/all_to_all | solution.py:20
  175.0 27.9 %copy.24 = bf16[16,4,150,600]{3,0,2,1:T(8,128)(2,1)} copy(bf16[16,4,150,600]{3,2,0,1:T(8,128)(2,1)} %bitcast.14) | data formatting | bytes 23040000 | tf_op jit(solution)/shard_map/all_to_all | solution.py:20
  202.9 23.4 %all-gather.8.cloned.1.call-done = bf16[8,45000,12]{1,2,0:T(8,128)(2,1)} async-done(((bf16[1,45000,12]{1,2,0:T(8,128)(2,1)}), bf16[8,45000,12]{1,2,0:T(8,128)(2,1)}) %all-gather.8.cloned.1.call-update) | async-done | bytes 8640016 | tf_op jit(solution)/shard_map/all_gather | solution.py:11
  226.4 13.7 %copy.20 = bf16[8,45000,12]{1,0,2:T(8,128)(2,1)} copy(bf16[8,45000,12]{1,2,0:T(8,128)(2,1)} %all-gather.8.cloned.1.call-done) | data formatting | bytes 17280000 | tf_op jit(solution)/shard_map/all_gather | solution.py:11
  240.1 34.1 %reshape.11 = bf16[360000,12]{0,1:T(8,128)(2,1)} reshape(bf16[8,45000,12]{1,0,2:T(8,128)(2,1)} %copy.20) | data formatting | bytes 17280000
  274.2 23.4 %reshape.15 = bf16[12,600,600,1]{2,1,0,3:T(8,128)(2,1)} reshape(bf16[12,360000]{1,0:T(8,128)(2,1)} %bitcast.66) | data formatting | bytes 17280000 | tf_op jit(solution)/shard_map/reshape | solution.py:12
  297.7 21.1 %fusion.24 = bf16[2,12,600,600]{2,3,1,0:T(8,128)(2,1)} fusion(bf16[12,600,600,1]{2,1,0,3:T(8,128)(2,1)} %reshape.15, bf16[1,2,600,600]{2,3,1,0:T(8,128)(2,1)S(1)} %copy.19), kind=kOutput, calls=%fused_computation.3.clone.clone.clone.1 | convolution fusion | flops 10376640512 | bytes 27360000 | tf_op jit(solution)/shard_map/qac,jcd->jqad/dot_general | solution.py:13
  318.8 112.4 %all-gather.10.cloned.1.call-done = bf16[8,150,9600]{2,1,0:T(8,128)(2,1)} async-done(((bf16[1,150,9600]{2,1,0:T(8,128)(2,1)}), bf16[8,150,9600]{2,1,0:T(8,128)(2,1)}) %all-gather.10.cloned.1.call-update) | async-done | bytes 23040016 | tf_op jit(solution)/shard_map/all_gather | solution.py:22
  431.2 24.2 %reshape.13 = bf16[1200,9600]{1,0:T(8,128)(2,1)} reshape(bf16[8,150,9600]{2,1,0:T(8,128)(2,1)} %all-gather.10.cloned.1.call-done) | data formatting | bytes 46080000
  455.4 49.1 %reshape.9 = bf16[16,600,1200]{1,0,2:T(8,128)(2,1)} reshape(bf16[9600,1200]{0,1:T(8,128)(2,1)} %bitcast.64) | data formatting | bytes 46080000 | tf_op jit(solution)/shard_map/reshape | solution.py:23
  504.5 24.8 %fusion = f32[600,2,600,1]{2,0,3,1:T(8,128)S(1)} fusion(bf16[2,600,600,16]{2,3,1,0:T(8,128)(2,1)} %bitcast.67, bf16[16,600,600]{2,0,1:T(8,128)(2,1)} %bitcast.68), kind=kOutput, calls=%fused_computation | convolution fusion | flops 13824000000 | bytes 37440000 | tf_op jit(solution)/shard_map/kac,kcn->an/dot_general | solution.py:24
  529.3 20.6 %bitcast_add_fusion = f32[600,2,600]{2,0,1:T(8,128)S(1)} fusion(f32[600,2,600,1]{2,0,3,1:T(8,128)S(1)} %fusion, bf16[12,600,600,1]{2,1,0,3:T(8,128)(2,1)} %reshape.15, bf16[2,12,600,600]{2,3,1,0:T(8,128)(2,1)} %fusion.24), kind=kOutput, calls=%fused_computation.8 | convolution fusion | flops 10368719872 | bytes 31680000 | tf_op jit(solution)/shard_map/jqad,qbd->ajb/dot_general | solution.py:16
  549.9 0.0 copy-start
  549.9 3.2 copy.27
  553.1 0.0 all-reduce.3.cloned.1.call-update
  553.1 0.0 copy-done
  553.1 0.6 dynamic-slice
  554.4 82.9 %all-reduce.3.cloned.1.call-done = f32[600,2,600]{2,1,0:T(2,128)} async-done(((f32[600,2,600]{2,1,0:T(2,128)}), f32[600,2,600]{2,1,0:T(2,128)}) %all-reduce.3.cloned.1.call-update) | async-done | bytes 2880016
  637.2 2.3 dynamic-slice_bitcast_fusion
Async XLA Ops:
  6.5 110.9 %all-gather.6.cloned.1.call-start = ((), (), s32[]{:S(2)}) async-start(), calls=%async_computation.1 | async-start | bytes 1920000 | tf_op jit(solution)/shard_map/all_gather | solution.py:10
  7.3 219.1 %all-gather.8.cloned.1.call-start = ((), (), s32[]{:S(2)}) async-start(), calls=%async_computation.2 | async-start | bytes 12976128 | tf_op jit(solution)/shard_map/all_gather | solution.py:11
  8.0 423.2 %all-gather.10.cloned.1.call-start = ((), (), s32[]{:S(2)}) async-start(), calls=%async_computation.3 | async-start | bytes 26265600 | tf_op jit(solution)/shard_map/all_gather | solution.py:22
  23.1 151.9 %all-to-all-start = ((bf16[64,150,600]{2,1,0:T(8,128)(2,1)}), bf16[64,150,600]{2,1,0:T(8,128)(2,1)}, u32[]{:S(2)}, u32[]{:S(2)}) async-start(bf16[64,150,600]{2,1,0:T(8,128)(2,1)} %bitcast.65), calls=%async_computation | async-start | bytes 24903680 | tf_op jit(solution)/shard_map/all_to_all | solution.py:20
  29.4 607.8 %all-reduce.3.cloned.1.call-start = ((), (), s32[]{:S(2)}) async-start(), calls=%async_computation.4 | async-start | bytes 6144000
  549.9 3.3 copy-start
Sparse Core Ops, SparseCore 0:
  9.2 108.2 all-gather.5
  119.1 107.2 all-gather.7
  228.0 203.1 all-gather.9
  553.2 83.9 all-reduce.2
where the time goes:
time: 651 us; the launch traced here: 646 us
  waiting for transfers between devices  362 us (56%)
  local copies, waits for them, and re-layouts  197 us (30%)
  matrix products  66.5 us (10%)
  between operations  14.3 us (2%)
  starting transfers between devices  6.7 us (1%)
    all_gather x1, waiting for transfers between devices, crossed_term(): piece = lax.all_gather(crossed_coupling, 'pair', axis=1, tiled=True)  112 us
    all_gather x1, waiting for transfers between devices, ladder_term(): pair_amps = lax.all_gather(amplitudes, 'orb', axis=2, tiled=True)  87.7 us
    unnamed x5, waiting for transfers between devices  85 us
    unnamed x6, local copies, waits for them, and re-layouts  73.2 us
    all_to_all x1, waiting for transfers between devices, crossed_term(): lax.all_to_all(crossed_amplitudes[0], 'orb', split_axis=0, concat_axis=1,...  53.8 us
    reshape x1, local copies, waits for them, and re-layouts, crossed_term(): block = piece.reshape(k_local, nvirt, piece.shape[1])  49.1 us
    all_to_all x1, local copies, waits for them, and re-layouts, crossed_term(): lax.all_to_all(crossed_amplitudes[0], 'orb', split_axis=0, concat_axis=1,...  27.9 us
    dot_general x1, matrix products, crossed_term(): jnp.einsum('kac,kcn->an', relaid, block, preferred_element_type=jnp.float32)  24.8 us
  transfers between devices with their start and end apart: 5, of which 5 were waited for; matrix products, arithmetic and copies ran while one was open for 22% of the time, Pallas kernels for 0%

commit v1 on v0

v1 whole, which is shorter than its diff:
```python
import jax
import jax.numpy as jnp
from jax import lax
from jax.sharding import Mesh, PartitionSpec as P

NV = 600
PAIR = ("zz", "core")


def pair_gather(x):
    g = lax.all_gather(x, "zz", axis=0, tiled=False)
    g = lax.all_gather(g, "core", axis=1, tiled=False)
    return g.reshape((g.shape[0] * g.shape[1],) + x.shape)


def ladder_term(amplitudes, factors, nvirt):
    nj = amplitudes.shape[1]
    t = lax.all_gather(amplitudes[0], "orb", axis=0, tiled=False)
    tm = t.transpose(0, 2, 1, 3).reshape(nvirt, nj * nvirt)
    g = pair_gather(factors)
    nq = factors.shape[0]
    cube = g.transpose(1, 0, 2).reshape(nq, nvirt, nvirt)
    inner = jnp.einsum("qac,cn->qan", cube, tm, preferred_element_type=jnp.float32).astype(jnp.bfloat16)
    inner = inner.reshape(nq, nvirt, nj, nvirt)
    return jnp.einsum("qajd,qbd->ajb", inner, cube, preferred_element_type=jnp.float32)


def crossed_term(crossed_amplitudes, crossed_coupling, nvirt, norb):
    ca = crossed_amplitudes[0]
    kocc, nva = ca.shape[0], ca.shape[1]
    kl = kocc // norb
    ca = ca.reshape(norb, kl, nva, nvirt)
    r = lax.all_to_all(ca, "orb", 0, 0, tiled=True)
    lhs = r.transpose(0, 2, 1, 3).reshape(norb * nva, kl * nvirt)
    w = pair_gather(crossed_coupling)
    product = jnp.einsum("ak,pkc->apc", lhs, w, preferred_element_type=jnp.float32)
    return product.reshape(nvirt, -1, nvirt)


def on_device(amplitudes, factors, crossed_amplitudes, crossed_coupling):
    nvirt = NV
    norb = lax.axis_size("orb")
    ladder = ladder_term(amplitudes, factors, nvirt)
    crossed = crossed_term(crossed_amplitudes, crossed_coupling, nvirt, norb)
    total = (ladder + crossed).reshape((norb, nvirt // norb) + ladder.shape[1:])
    total = lax.psum_scatter(total, "orb", scatter_dimension=0, tiled=True)
    return total


def solution(mesh):
    npair, norb = mesh.shape["pair"], mesh.shape["orb"]
    sub = Mesh(mesh.devices.reshape(npair // 2, 2, norb), ("zz", "core", "orb"))
    return jax.shard_map(
        on_device,
        mesh=sub,
        in_specs=(
            P(PAIR, None, "orb", None),
            P("orb", PAIR),
            P(PAIR, None, "orb", None),
            P("orb", PAIR),
        ),
        out_specs=P(PAIR, "orb", None, None),
        check_vma=False,
    )
```

time: 651 us -> 875 us (1.34)
  waiting for transfers between devices: 362 us -> 520 us
  local copies, waits for them, and re-layouts: 197 us -> 261 us
    all_gather x3 -> x5, waiting for transfers between devices: 224 us -> 305 us  [the longest x2 305 us: pair_gather(): g = lax.all_gather(x, 'zz', axis=0, tiled=False)]
    all_to_all x1, waiting for transfers between devices: 53.8 us -> 130 us  [crossed_term(): r = lax.all_to_all(ca, 'orb', 0, 0, tiled=True)]
    reshape x2 -> x8, local copies, waits for them, and re-layouts: 72.5 us -> 148 us  [the longest x2 43.6 us: pair_gather(): return g.reshape((g.shape[0] * g.shape[1],) + x.shape)]
    unnamed x6 -> x4, local copies, waits for them, and re-layouts: 73.2 us -> 3.49 us
    dot_general x0 -> x2, local copies, waits for them, and re-layouts: none -> 46.7 us  [crossed_term(): jnp.einsum('ak,pkc->apc', lhs, w, preferred_element_type=jnp.float32)]
    all_to_all x1 -> x0, local copies, waits for them, and re-layouts: 27.9 us -> none  [crossed_term(): lax.all_to_all(crossed_amplitudes[0], 'orb', split_axis=0, concat_axis=1,...]
    all_gather x2 -> x3, local copies, waits for them, and re-layouts: 17.5 us -> 40 us  [the longest x2 28.5 us: pair_gather(): g = lax.all_gather(x, 'zz', axis=0, tiled=False)]
    transpose x0 -> x1, local copies, waits for them, and re-layouts: none -> 12.3 us  [ladder_term(): cube = g.transpose(1, 0, 2).reshape(nq, nvirt, nvirt)]
  transfers between devices with their start and end apart: 5 -> 7, of which waited for: 5 -> 4; matrix products, arithmetic and copies ran while one was open for 22% -> 22% of each run, Pallas kernels for 0% -> 0%
where the time goes in v1:
time: 875 us; the launch traced here: 866 us
  waiting for transfers between devices  520 us (59%)
  local copies, waits for them, and re-layouts  261 us (30%)
  matrix products  64.3 us (7%)
  between operations  13.8 us (2%)
    all_gather x2, waiting for transfers between devices, pair_gather(): g = lax.all_gather(x, 'zz', axis=0, tiled=False)  305 us
    all_to_all x1, waiting for transfers between devices, crossed_term(): r = lax.all_to_all(ca, 'orb', 0, 0, tiled=True)  130 us
    unnamed x7, waiting for transfers between devices  84.7 us
    dot_general x2, local copies, waits for them, and re-layouts, crossed_term(): jnp.einsum('ak,pkc->apc', lhs, w, preferred_element_type=jnp.float32)  46.7 us
    reshape x2, local copies, waits for them, and re-layouts, pair_gather(): return g.reshape((g.shape[0] * g.shape[1],) + x.shape)  43.6 us
    reshape x1, local copies, waits for them, and re-layouts, ladder_term(): inner = inner.reshape(nq, nvirt, nj, nvirt)  40.3 us
    reshape x2, local copies, waits for them, and re-layouts, ladder_term(): cube = g.transpose(1, 0, 2).reshape(nq, nvirt, nvirt)  37.4 us
    all_gather x2, local copies, waits for them, and re-layouts, pair_gather(): g = lax.all_gather(x, 'zz', axis=0, tiled=False)  28.5 us
  transfers between devices with their start and end apart: 7, of which 4 were waited for; matrix products, arithmetic and copies ran while one was open for 22% of the time, Pallas kernels for 0%

profile of v1, /device:TPU:0, one launch (start us, length us, event | category | flops | bytes accessed | tf_op | source)
XLA Modules:
  0.0 865.8 jit_solution(5914454755707076784)
XLA Ops:
  6.5 0.0 all-gather.19.cloned.1.call-start
  6.5 0.7 all-gather.19.cloned.1.call-update
  7.3 0.0 all-gather.15.cloned.1.call-start
  7.3 0.7 all-gather.15.cloned.1.call-update
  8.0 0.0 all-gather.11.cloned.1.call-start
  8.1 0.7 all-gather.11.cloned.1.call-update
  8.7 0.0 all-gather.13.cloned.1.call-start
  8.8 109.6 %all-gather.19.cloned.1.call-done = bf16[4,12,45000]{2,1,0:T(8,128)(2,1)} async-done(((bf16[1,12,45000]{2,1,0:T(8,128)(2,1)}), bf16[4,12,45000]{2,1,0:T(8,128)(2,1)}) %all-gather.19.cloned.1.call-update) | async-done | bytes 4320016 | tf_op jit(solution)/shard_map/all_gather | solution.py:11
  118.3 8.1 copy.14
  126.5 0.0 all-gather.13.cloned.1.call-update
  126.5 0.0 all-gather.17.cloned.1.call-start
  126.5 195.0 %all-gather.15.cloned.1.call-done = bf16[38400,150]{0,1:T(8,128)(2,1)} async-done(((bf16[9600,150]{0,1:T(8,128)(2,1)}), bf16[38400,150]{0,1:T(8,128)(2,1)}) %all-gather.15.cloned.1.call-update) | async-done | bytes 11520016 | tf_op jit(solution)/shard_map/all_gather | solution.py:11
  321.5 20.3 %reshape.32 = bf16[4,9600,150]{1,0,2:T(4,128)(2,1)} reshape(bf16[38400,150]{0,1:T(8,128)(2,1)} %all-gather.15.cloned.1.call-done) | data formatting | bytes 23040000 | tf_op jit(solution)/shard_map/all_gather | solution.py:11
  341.9 0.0 all-gather.17.cloned.1.call-update
  341.9 10.4 %copy.18 = bf16[4,16,150,600]{3,1,2,0:T(8,128)(2,1)} copy(bf16[4,16,150,600]{3,1,0,2:T(8,128)(2,1)} %bitcast.24) | data formatting | bytes 23040000 | tf_op jit(solution)/shard_map/reshape;squeeze | solution.py:32
  352.3 6.3 all-to-all-start
  358.7 0.6 all-reduce.3.cloned.1.call-start
  359.2 0.0 all-gather.11.cloned.1.call-done
  359.3 3.7 reshape.39
  362.9 130.3 %all-to-all-done = bf16[4,16,150,600]{3,1,2,0:T(8,128)(2,1)} async-done(((bf16[4,16,150,600]{3,1,2,0:T(8,128)(2,1)}), bf16[4,16,150,600]{3,1,2,0:T(8,128)(2,1)}, u32[]{:S(2)}, u32[]{:S(2)}) %all-to-all-start) | async-done | bytes 11520032 | tf_op jit(solution)/shard_map/all_to_all | solution.py:33
  493.2 20.0 %reshape.42 = bf16[600,9600,1]{1,0,2:T(8,128)(2,1)} reshape(bf16[4,150,16,600]{3,2,1,0:T(8,128)(2,1)} %bitcast.6) | data formatting | bytes 23040000 | tf_op jit(solution)/shard_map/reshape | solution.py:34
  513.2 0.0 all-gather.13.cloned.1.call-done
  513.2 11.6 %copy.15 = bf16[4,24,45000]{2,1,0:T(8,128)(2,1)} copy(bf16[4,24,45000]{2,0,1:T(4,128)(2,1)} %all-gather.13.cloned.1.call-done) | data formatting | bytes 17280000 | tf_op jit(solution)/shard_map/all_gather | solution.py:12
  524.8 9.0 %reshape.23 = bf16[8,12,45000]{2,1,0:T(8,128)(2,1)} reshape(bf16[4,24,45000]{2,1,0:T(8,128)(2,1)} %copy.15) | data formatting | bytes 17280000 | tf_op jit(solution)/shard_map/reshape | solution.py:13
  533.7 12.3 %copy.16 = bf16[12,8,45000]{2,1,0:T(8,128)(2,1)} copy(bf16[12,8,45000]{2,0,1:T(8,128)(2,1)} %bitcast.23) | data formatting | bytes 17280000 | tf_op jit(solution)/shard_map/transpose | solution.py:22
  546.1 18.7 %reshape.40 = bf16[12,600,600,1]{2,1,0,3:T(8,128)(2,1)} reshape(bf16[12,8,45000]{2,1,0:T(8,128)(2,1)} %copy.16) | data formatting | bytes 17280000 | tf_op jit(solution)/shard_map/reshape | solution.py:22
  564.8 18.7 %reshape.24 = bf16[12,600,600]{2,1,0:T(8,128)(2,1)} reshape(bf16[12,8,45000]{2,1,0:T(8,128)(2,1)} %copy.16) | data formatting | bytes 17280000 | tf_op jit(solution)/shard_map/reshape | solution.py:22
  583.4 21.0 %convolution_convert_fusion = bf16[12,600,1200]{2,1,0:T(8,128)(2,1)} fusion(bf16[12,600,600]{2,1,0:T(8,128)(2,1)} %reshape.24, bf16[600,1200,1]{1,0,2:T(8,128)(2,1)S(1)} %reshape.39), kind=kOutput, calls=%fused_computation | convolution fusion | flops 10376640512 | bytes 27360000 | tf_op jit(solution)/shard_map/qac,cn->qan/dot_general | solution.py:23
  604.5 40.3 %reshape.26 = bf16[12,600,2,600]{3,2,1,0:T(2,128)(2,1)} reshape(bf16[12,600,1200]{2,1,0:T(8,128)(2,1)} %convolution_convert_fusion) | data formatting | bytes 34560000 | tf_op jit(solution)/shard_map/reshape | solution.py:24
  644.7 0.0 all-gather.17.cloned.1.call-done
  644.7 34.7 %reshape.28 = bf16[8,9600,150]{1,0,2:T(8,128)(2,1)} reshape(bf16[4,19200,150]{1,0,2:T(4,128)(2,1)} %all-gather.17.cloned.1.call-done) | data formatting | bytes 46080000 | tf_op jit(solution)/shard_map/reshape | solution.py:13
  679.4 22.6 %copy.19 = bf16[8,150,9600]{2,1,0:T(8,128)(2,1)} copy(bf16[8,150,9600]{2,0,1:T(8,128)(2,1)} %bitcast.22) | data formatting | bytes 46080000 | tf_op jit(solution)/shard_map/ak,pkc->apc/dot_general | solution.py:36
  702.1 24.1 %dot_general.16 = bf16[2,600,9600]{2,1,0:T(8,128)(2,1)} reshape(bf16[8,150,9600]{2,1,0:T(8,128)(2,1)} %copy.19) | data formatting | bytes 46080000 | tf_op jit(solution)/shard_map/ak,pkc->apc/dot_general | solution.py:36
  726.1 22.2 %fusion.4 = f32[600,2,600]{2,0,1:T(8,128)} fusion(bf16[600,9600,1]{1,0,2:T(8,128)(2,1)} %reshape.42, bf16[2,600,9600]{2,1,0:T(8,128)(2,1)} %dot_general.16), kind=kOutput, calls=%fused_computation.5 | convolution fusion | flops 13824000000 | bytes 37440000 | tf_op jit(solution)/shard_map/ak,pkc->apc/dot_general | solution.py:36
  748.3 21.1 %bitcast_add_fusion = f32[600,2,600]{2,0,1:T(8,128)S(1)} fusion(f32[600,2,600]{2,0,1:T(8,128)} %fusion.4, bf16[12,600,600,1]{2,1,0,3:T(8,128)(2,1)} %reshape.40, bf16[12,600,2,600]{3,2,1,0:T(2,128)(2,1)} %reshape.26), kind=kOutput, calls=%fused_computation.3 | convolution fusion | flops 10368719872 | bytes 31680000 | tf_op jit(solution)/shard_map/qajd,qbd->ajb/dot_general | solution.py:25
  769.4 0.0 copy-start
  769.4 3.2 copy.22
  772.6 0.0 all-reduce.3.cloned.1.call-update
  772.7 0.0 copy-done
  772.7 0.6 dynamic-slice
  773.3 82.5 %all-reduce.3.cloned.1.call-done = f32[4,150,2,600]{3,2,1,0:T(2,128)} async-done(((f32[4,150,2,600]{3,2,1,0:T(2,128)}), f32[4,150,2,600]{3,2,1,0:T(2,128)}) %all-reduce.3.cloned.1.call-update) | async-done | bytes 2880016
  855.8 2.9 constant_dynamic-slice_fusion
Async XLA Ops:
  6.5 111.8 %all-gather.19.cloned.1.call-start = ((), (), s32[]{:S(2)}) async-start(), calls=%async_computation.5 | async-start | bytes 7208960 | tf_op jit(solution)/shard_map/all_gather | solution.py:11
  7.3 314.3 %all-gather.15.cloned.1.call-start = ((), (), s32[]{:S(2)}) async-start(), calls=%async_computation.3 | async-start | bytes 14592000 | tf_op jit(solution)/shard_map/all_gather | solution.py:11
  8.0 351.3 %all-gather.11.cloned.1.call-start = ((), (), s32[]{:S(2)}) async-start(), calls=%async_computation.1 | async-start | bytes 1920000 | tf_op jit(solution)/shard_map/all_gather | solution.py:18
  8.7 504.5 %all-gather.13.cloned.1.call-start = ((), (), s32[]{:S(2)}) async-start(), calls=%async_computation.2 | async-start | bytes 12976128 | tf_op jit(solution)/shard_map/all_gather | solution.py:12
  126.5 518.2 %all-gather.17.cloned.1.call-start = ((), (), s32[]{:S(2)}) async-start(), calls=%async_computation.4 | async-start | bytes 34560000 | tf_op jit(solution)/shard_map/all_gather | solution.py:12
  352.3 140.9 %all-to-all-start = ((bf16[4,16,150,600]{3,1,2,0:T(8,128)(2,1)}), bf16[4,16,150,600]{3,1,2,0:T(8,128)(2,1)}, u32[]{:S(2)}, u32[]{:S(2)}) async-start(bf16[4,16,150,600]{3,1,2,0:T(8,128)(2,1)} %copy.18), calls=%async_computation | async-start | bytes 24576000 | tf_op jit(solution)/shard_map/all_to_all | solution.py:33
  358.7 497.2 %all-reduce.3.cloned.1.call-start = ((), (), s32[]{:S(2)}) async-start(), calls=%async_computation.6 | async-start | bytes 6144000
  769.4 3.3 copy-start
Sparse Core Ops, SparseCore 0:
  8.9 109.3 all-gather.18
  119.9 201.5 all-gather.14
  323.4 28.7 all-gather.10
  353.6 20.8 all-gather.12
  375.9 38.7 all-gather.16
  772.8 82.9 all-reduce.2

commit v2 on v1

v2 whole, which is shorter than its diff:
```python
import jax
import jax.numpy as jnp
from jax import lax
from jax.sharding import Mesh, PartitionSpec as P

NV = 600
PAIR = ("zz", "core")


def relay(x, n):
    zz = lax.axis_index("zz")
    out = [(x, zz)]
    right, left = x, x
    for s in range(1, n):
        right = lax.ppermute(right, "zz", [(i, i + 1) for i in range(s - 1, n - 1)])
        left = lax.ppermute(left, "zz", [(j, j - 1) for j in range(1, n - s + 1)])
        out.append((right, jnp.maximum(zz - s, 0)))
        out.append((left, jnp.minimum(zz + s, n - 1)))
    return out


def ladder_term(amplitudes, factors, nvirt):
    nj = amplitudes.shape[1]
    t = lax.all_gather(amplitudes[0], "orb", axis=0, tiled=False)
    tm = t.transpose(0, 2, 1, 3).reshape(nvirt, nj * nvirt)
    g = lax.all_gather(factors, PAIR, axis=0, tiled=False)
    nq = factors.shape[0]
    cube = g.transpose(1, 0, 2).reshape(nq, nvirt, nvirt)
    inner = jnp.einsum("qac,cn->qan", cube, tm, preferred_element_type=jnp.float32).astype(jnp.bfloat16)
    inner = inner.reshape(nq, nvirt, nj, nvirt)
    return jnp.einsum("qajd,qbd->ajb", inner, cube, preferred_element_type=jnp.float32)


def crossed_term(crossed_amplitudes, crossed_coupling, nvirt, norb, nchip):
    ca = crossed_amplitudes[0]
    kocc, nva = ca.shape[0], ca.shape[1]
    kl = kocc // norb
    ca = ca.reshape(norb, kl, nva, nvirt)
    r = lax.all_to_all(ca, "orb", 0, 0, tiled=True)
    lhs = r.transpose(0, 2, 1, 3).reshape(norb * nva, kl * nvirt)
    wt = crossed_coupling.T
    ncol = wt.shape[0]
    core = lax.axis_index("core")
    out = jnp.zeros((lhs.shape[0], 2 * nchip, ncol), jnp.float32)
    for block, origin in relay(wt, nchip):
        other = lax.ppermute(block, "core", [(0, 1), (1, 0)])
        for b, c in ((block, core), (other, 1 - core)):
            part = jnp.einsum("ak,nk->an", lhs, b, preferred_element_type=jnp.float32)
            at = 2 * origin + c
            cur = lax.dynamic_slice_in_dim(out, at, 1, axis=1)
            out = lax.dynamic_update_slice_in_dim(out, cur + part[:, None], at, axis=1)
    return out.reshape(nvirt, -1, nvirt)


def on_device(amplitudes, factors, crossed_amplitudes, crossed_coupling):
    nvirt = NV
    norb = lax.axis_size("orb")
    nchip = lax.axis_size("zz")
    ladder = ladder_term(amplitudes, factors, nvirt)
    crossed = crossed_term(crossed_amplitudes, crossed_coupling, nvirt, norb, nchip)
    total = (ladder + crossed).reshape((norb, nvirt // norb) + ladder.shape[1:])
    return lax.psum_scatter(total, "orb", scatter_dimension=0, tiled=True)


def solution(mesh):
    npair, norb = mesh.shape["pair"], mesh.shape["orb"]
    sub = Mesh(mesh.devices.reshape(npair // 2, 2, norb), ("zz", "core", "orb"))
    return jax.shard_map(
        on_device,
        mesh=sub,
        in_specs=(
            P(PAIR, None, "orb", None),
            P("orb", PAIR),
            P(PAIR, None, "orb", None),
            P("orb", PAIR),
        ),
        out_specs=P(PAIR, "orb", None, None),
        check_vma=False,
    )
```

time: 875 us -> 629 us (0.72)
  waiting for transfers between devices: 520 us -> 324 us
  local copies, waits for them, and re-layouts: 261 us -> 138 us
  matrix products: 64.3 us -> 123 us
  starting transfers between devices: 7.05 us -> 22.2 us
    all_gather x4 -> x1, waiting for transfers between devices: 305 us -> 0.02 us  [ladder_term(): g = lax.all_gather(factors, PAIR, axis=0, tiled=False)]
    ppermute x0 -> x13, waiting for transfers between devices: none -> 157 us  [the longest x3 97 us: relay(): left = lax.ppermute(left, 'zz', [(j, j - 1) for j in range(1, n - s + 1)])]
    all_to_all x1, waiting for transfers between devices: 130 us -> 0.01 us  [crossed_term(): r = lax.all_to_all(ca, 'orb', 0, 0, tiled=True)]
    all_gather x1, waiting for transfers between devices: 0.02 us -> 81.4 us  [ladder_term(): t = lax.all_gather(amplitudes[0], 'orb', axis=0, tiled=False)]
    dot_general x1 -> x14, matrix products: 22.2 us -> 80.2 us  [crossed_term(): part = jnp.einsum('ak,nk->an', lhs, b, preferred_element_type=jnp.float32)]
    dot_general x2 -> x0, local copies, waits for them, and re-layouts: 46.7 us -> none  [crossed_term(): jnp.einsum('ak,pkc->apc', lhs, w, preferred_element_type=jnp.float32)]
    all_gather x3 -> x0, local copies, waits for them, and re-layouts: 40 us -> none  [the longest x2 28.5 us: pair_gather(): g = lax.all_gather(x, 'zz', axis=0, tiled=False)]
    reshape x2, local copies, waits for them, and re-layouts: 43.6 us -> 4.46 us  [crossed_term(): return out.reshape(nvirt, -1, nvirt)]
  transfers between devices with their start and end apart: 7 -> 17, of which waited for: 4 -> 5; matrix products, arithmetic and copies ran while one was open for 22% -> 18% of each run, Pallas kernels for 0% -> 0%
where the time goes in v2:
time: 629 us; the launch traced here: 621 us
  waiting for transfers between devices  324 us (52%)
  local copies, waits for them, and re-layouts  138 us (22%)
  matrix products  123 us (20%)
  starting transfers between devices  22.2 us (4%)
  between operations  13.6 us (2%)
    ppermute x3, waiting for transfers between devices, relay(): left = lax.ppermute(left, 'zz', [(j, j - 1) for j in range(1, n - s + 1)])  97 us
    unnamed x4, waiting for transfers between devices  85.7 us
    all_gather x1, waiting for transfers between devices, ladder_term(): t = lax.all_gather(amplitudes[0], 'orb', axis=0, tiled=False)  81.4 us
    dot_general x14, matrix products, crossed_term(): part = jnp.einsum('ak,nk->an', lhs, b, preferred_element_type=jnp.float32)  80.2 us
    ppermute x3, waiting for transfers between devices, relay(): right = lax.ppermute(right, 'zz', [(i, i + 1) for i in range(s - 1, n - 1)])  59.9 us
    reshape x1, local copies, waits for them, and re-layouts, ladder_term(): inner = inner.reshape(nq, nvirt, nj, nvirt)  40.1 us
    reshape x2, local copies, waits for them, and re-layouts, ladder_term(): cube = g.transpose(1, 0, 2).reshape(nq, nvirt, nvirt)  37.3 us
    dot_general x1, matrix products, ladder_term(): jnp.einsum('qac,cn->qan', cube, tm, preferred_element_type=jnp.float32)  21.7 us
  transfers between devices with their start and end apart: 17, of which 5 were waited for; matrix products, arithmetic and copies ran while one was open for 18% of the time, Pallas kernels for 0%

profile of v2, /device:TPU:0, one launch (start us, length us, event | category | flops | bytes accessed | tf_op | source)
XLA Modules:
  0.0 621.5 jit_solution(10608588924570776095)
XLA Ops:
  6.5 10.4 %copy.15 = bf16[4,16,150,600]{3,1,2,0:T(8,128)(2,1)} copy(bf16[4,16,150,600]{3,1,0,2:T(8,128)(2,1)} %bitcast.92) | data formatting | bytes 23040000 | tf_op jit(solution)/shard_map/reshape;squeeze | solution.py:38
  16.9 6.4 %all-to-all-start = ((bf16[4,16,150,600]{3,1,2,0:T(8,128)(2,1)}), bf16[4,16,150,600]{3,1,2,0:T(8,128)(2,1)}, u32[]{:S(2)}, u32[]{:S(2)}) async-start(bf16[4,16,150,600]{3,1,2,0:T(8,128)(2,1)} %copy.15), calls=%async_computation | async-start | bytes 24576000 | tf_op jit(solution)/shard_map/all_to_all | solution.py:39
  23.3 6.5 %collective-permute-start.1 = (bf16[150,9600]{1,0:T(8,128)(2,1)}, bf16[150,9600]{1,0:T(8,128)(2,1)}, u32[]{:S(2)}, u32[]{:S(2)}) collective-permute-start(bf16[150,9600]{1,0:T(8,128)(2,1)} %bitcast.8), channel_id=1, source_target_pairs={{0,8},{8,16},{16,24},{1,9},{9,17},{17,25},{2,10},{10,18},{18,26},{... | collective-permute-start | bytes 8640008 | tf_op jit(solution)/shard_map/ppermute | solution.py:15
  29.9 1.3 collective-permute-start.3
  31.2 59.9 %collective-permute-done.1 = bf16[150,9600]{1,0:T(8,128)(2,1)} collective-permute-done((bf16[150,9600]{1,0:T(8,128)(2,1)}, bf16[150,9600]{1,0:T(8,128)(2,1)}, u32[]{:S(2)}, u32[]{:S(2)}) %collective-permute-start.1) | collective-permute-done | bytes 2880032 | tf_op jit(solution)/shard_map/ppermute | solution.py:15
  91.1 2.2 collective-permute-start.5
  93.3 0.0 all-gather.7.cloned.1.call-start
  93.4 0.1 collective-permute-start
  93.4 3.3 collective-permute-done.3
  96.8 1.3 collective-permute-start.7
  98.1 0.0 all-reduce.3.cloned.1.call-start
  98.2 81.4 %all-gather.5.cloned.1.call-done = bf16[4,2,150,600]{3,1,2,0:T(2,128)(2,1)} async-done(((bf16[1,2,150,600]{3,1,2,0:T(2,128)(2,1)}), bf16[4,2,150,600]{3,1,2,0:T(2,128)(2,1)}) %all-gather.5.cloned.1.call-update) | async-done | bytes 1440016 | tf_op jit(solution)/shard_map/all_gather | solution.py:24
  179.6 4.5 reshape.28
  184.0 0.5 collective-permute-start.4
  184.6 20.2 %reshape.21 = bf16[600,9600]{1,0:T(8,128)(2,1)} reshape(bf16[4,150,16,600]{3,2,1,0:T(8,128)(2,1)} %bitcast.6) | data formatting | bytes 23040000 | tf_op jit(solution)/shard_map/reshape | solution.py:40
  204.8 0.2 broadcast_in_dim.45
  205.0 7.6 %fusion.4 = f32[600,8,150]{0,2,1:T(8,128)S(1)} fusion(f32[600,8,150]{0,2,1:T(8,128)S(1)} %broadcast_in_dim.45, s32[]{:T(128)S(6)} %select_n.55, bf16[600,9600]{1,0:T(8,128)(2,1)} %reshape.21, bf16[9600,150]{0,1:T(8,128)(2,1)} %param.7), kind=kOutput, calls=%fused_computation.18 | convolution fusion | flops 1728000000 | bytes 14789124 | tf_op jit(solution)/shard_map/ak,nk->an/dot_general | solution.py:48
  212.6 1.3 collective-permute-start.9
  213.9 0.5 collective-permute-start.8
  214.4 6.2 %fusion.6 = f32[600,8,150]{0,2,1:T(8,128)S(1)} fusion(f32[600,8,150]{0,2,1:T(8,128)S(1)} %fusion.4, s32[]{:T(128)S(6)} %select_n.56, bf16[600,9600]{1,0:T(8,128)(2,1)S(1)} %copy-done, bf16[150,9600]{1,0:T(8,128)(2,1)} %collective-permute-done), kind=kOutput, calls=%fused_computation.20 | convolution fusion | flops 1728089984 | bytes 15178244 | tf_op jit(solution)/shard_map/ak,nk->an/dot_general | solution.py:48
  220.7 6.3 %add_dynamic-update-slice_fusion.8 = f32[600,8,150]{0,2,1:T(8,128)S(1)} fusion(f32[600,8,150]{0,2,1:T(8,128)S(1)} %fusion.6, s32[]{:T(128)S(6)} %select_n.57, bf16[600,9600]{1,0:T(8,128)(2,1)S(1)} %copy-done, bf16[150,9600]{1,0:T(8,128)(2,1)} %collective-permute-done.1), kind=kOutput, calls=%fused_computation.35 | convolution fusion | flops 1728089984 | bytes 15178244 | tf_op jit(solution)/shard_map/ak,nk->an/dot_general | solution.py:48
  227.0 1.8 collective-permute-start.11
  228.8 6.3 %fusion.8 = f32[600,8,150]{0,2,1:T(8,128)S(1)} fusion(f32[600,8,150]{0,2,1:T(8,128)S(1)} %add_dynamic-update-slice_fusion.8, s32[]{:T(128)S(6)} %select_n.58, bf16[600,9600]{1,0:T(8,128)(2,1)S(1)} %copy-done, bf16[150,9600]{1,0:T(8,128)(2,1)} %collective-permute-done.2), kind=kOutput, calls=%fused_computation.22 | convolution fusion | flops 1728089984 | bytes 15178244 | tf_op jit(solution)/shard_map/ak,nk->an/dot_general | solution.py:48
  235.1 6.3 %add_dynamic-update-slice_fusion.7 = f32[600,8,150]{0,2,1:T(8,128)S(1)} fusion(f32[600,8,150]{0,2,1:T(8,128)S(1)} %fusion.8, s32[]{:T(128)S(6)} %select_n.59, bf16[600,9600]{1,0:T(8,128)(2,1)S(1)} %copy-done, bf16[150,9600]{1,0:T(8,128)(2,1)} %collective-permute-done.3), kind=kOutput, calls=%fused_computation.34 | convolution fusion | flops 1728089984 | bytes 15178244 | tf_op jit(solution)/shard_map/ak,nk->an/dot_general | solution.py:48
  241.4 6.4 %add_dynamic-update-slice_fusion.6 = f32[600,8,150]{0,2,1:T(8,128)S(1)} fusion(f32[600,8,150]{0,2,1:T(8,128)S(1)} %add_dynamic-update-slice_fusion.7, s32[]{:T(128)S(6)} %select_n.60, bf16[600,9600]{1,0:T(8,128)(2,1)S(1)} %copy-done, bf16[150,9600]{1,0:T(8,128)(2,1)} %collective-permute-done.4), kind=kOutput, calls=%fused_computation.33 | convolution fusion | flops 1728089984 | bytes 15178244 | tf_op jit(solution)/shard_map/ak,nk->an/dot_general | solution.py:48
  247.8 6.2 %add_dynamic-update-slice_fusion.5 = f32[600,8,150]{0,2,1:T(8,128)S(1)} fusion(f32[600,8,150]{0,2,1:T(8,128)S(1)} %add_dynamic-update-slice_fusion.6, s32[]{:T(128)S(6)} %select_n.61, bf16[600,9600]{1,0:T(8,128)(2,1)S(1)} %copy-done, bf16[150,9600]{1,0:T(8,128)(2,1)} %collective-permute-done.5), kind=kOutput, calls=%fused_computation.32 | convolution fusion | flops 1728089984 | bytes 15178244 | tf_op jit(solution)/shard_map/ak,nk->an/dot_general | solution.py:48
  254.1 0.1 collective-permute-start.10
  254.1 93.7 %collective-permute-done.11 = bf16[150,9600]{1,0:T(8,128)(2,1)S(1)} collective-permute-done((bf16[150,9600]{1,0:T(8,128)(2,1)}, bf16[150,9600]{1,0:T(8,128)(2,1)S(1)}, u32[]{:S(2)}, u32[]{:S(2)}) %collective-permute-start.11) | collective-permute-done | bytes 2880032 | tf_op jit(solution)/shard_map/ppermute | solution.py:16
  347.9 0.1 collective-permute-start.12
  348.0 6.4 %fusion.10 = f32[600,8,150]{0,2,1:T(8,128)S(1)} fusion(f32[600,8,150]{0,2,1:T(8,128)S(1)} %add_dynamic-update-slice_fusion.5, s32[]{:T(128)S(6)} %select_n.62, bf16[600,9600]{1,0:T(8,128)(2,1)S(1)} %copy-done, bf16[150,9600]{1,0:T(8,128)(2,1)} %collective-permute-done.6), kind=kOutput, calls=%fused_computation.24 | convolution fusion | flops 1728089984 | bytes 15178244 | tf_op jit(solution)/shard_map/ak,nk->an/dot_general | solution.py:48
  354.4 6.2 %add_dynamic-update-slice_fusion.4 = f32[600,8,150]{0,2,1:T(8,128)S(1)} fusion(f32[600,8,150]{0,2,1:T(8,128)S(1)} %fusion.10, s32[]{:T(128)S(6)} %select_n.63, bf16[600,9600]{1,0:T(8,128)(2,1)S(1)} %copy-done, bf16[150,9600]{1,0:T(8,128)(2,1)} %collective-permute-done.7), kind=kOutput, calls=%fused_computation.31 | convolution fusion | flops 1728089984 | bytes 15178244 | tf_op jit(solution)/shard_map/ak,nk->an/dot_general | solution.py:48
  360.6 4.4 add_dynamic-update-slice_fusion.3
  365.0 4.4 add_dynamic-update-slice_fusion.2
  369.5 4.6 fusion.12
  374.1 4.4 add_dynamic-update-slice_fusion.1
  378.5 4.4 add_dynamic-update-slice_fusion
  382.9 2.1 reshape.22
  385.0 2.4 copy.16
  387.4 12.4 %copy.13 = bf16[12,8,45000]{2,1,0:T(8,128)(2,1)} copy(bf16[12,8,45000]{2,0,1:T(8,128)(2,1)} %bitcast.94) | data formatting | bytes 17280000 | tf_op jit(solution)/shard_map/transpose | solution.py:28
  399.8 18.7 %reshape.18 = bf16[12,600,600]{2,1,0:T(8,128)(2,1)} reshape(bf16[12,8,45000]{2,1,0:T(8,128)(2,1)} %copy.13) | data formatting | bytes 17280000 | tf_op jit(solution)/shard_map/reshape | solution.py:28
  418.4 18.7 %reshape.29 = bf16[12,600,600,1]{2,1,0,3:T(8,128)(2,1)} reshape(bf16[12,8,45000]{2,1,0:T(8,128)(2,1)} %copy.13) | data formatting | bytes 17280000 | tf_op jit(solution)/shard_map/reshape | solution.py:28
  437.1 21.7 %convolution_convert_fusion = bf16[12,600,1200]{2,1,0:T(8,128)(2,1)} fusion(bf16[12,600,600]{2,1,0:T(8,128)(2,1)} %reshape.18, bf16[600,1200,1]{1,0,2:T(8,128)(2,1)} %reshape.28), kind=kOutput, calls=%fused_computation | convolution fusion | flops 10376640512 | bytes 27360000 | tf_op jit(solution)/shard_map/qac,cn->qan/dot_general | solution.py:29
  458.8 40.1 %reshape.20 = bf16[12,600,2,600]{3,2,1,0:T(2,128)(2,1)} reshape(bf16[12,600,1200]{2,1,0:T(8,128)(2,1)} %convolution_convert_fusion) | data formatting | bytes 34560000 | tf_op jit(solution)/shard_map/reshape | solution.py:30
  498.9 21.6 %bitcast_add_fusion = f32[600,2,600]{2,0,1:T(8,128)} fusion(f32[600,2,600]{2,0,1:T(8,128)S(1)} %copy.16, bf16[12,600,600,1]{2,1,0,3:T(8,128)(2,1)} %reshape.29, bf16[12,600,2,600]{3,2,1,0:T(2,128)(2,1)} %reshape.20), kind=kOutput, calls=%fused_computation.3 | convolution fusion | flops 10368719872 | bytes 31680000 | tf_op jit(solution)/shard_map/qajd,qbd->ajb/dot_general | solution.py:31
  520.5 5.1 copy.19
  525.6 0.6 dynamic-slice
  526.2 85.7 %all-reduce.3.cloned.1.call-done = f32[4,150,2,600]{3,2,1,0:T(2,128)} async-done(((f32[4,150,2,600]{3,2,1,0:T(2,128)}), f32[4,150,2,600]{3,2,1,0:T(2,128)}) %all-reduce.3.cloned.1.call-update) | async-done | bytes 2880016
  611.9 2.9 constant_dynamic-slice_fusion
  (22 shorter events, 0.2 us)
Async XLA Ops:
  16.9 167.7 %all-to-all-start = ((bf16[4,16,150,600]{3,1,2,0:T(8,128)(2,1)}), bf16[4,16,150,600]{3,1,2,0:T(8,128)(2,1)}, u32[]{:S(2)}, u32[]{:S(2)}) async-start(bf16[4,16,150,600]{3,1,2,0:T(8,128)(2,1)} %copy.15), calls=%async_computation | async-start | bytes 24576000 | tf_op jit(solution)/shard_map/all_to_all | solution.py:39
  23.3 156.3 %all-gather.5.cloned.1.call-start = ((), (), s32[]{:S(2)}) async-start(), calls=%async_computation.1 | async-start | bytes 1920000 | tf_op jit(solution)/shard_map/all_gather | solution.py:24
  23.3 67.8 %collective-permute-start.1 = (bf16[150,9600]{1,0:T(8,128)(2,1)}, bf16[150,9600]{1,0:T(8,128)(2,1)}, u32[]{:S(2)}, u32[]{:S(2)}) collective-permute-start(bf16[150,9600]{1,0:T(8,128)(2,1)} %bitcast.8), channel_id=1, source_target_pairs={{0,8},{8,16},{16,24},{1,9},{9,17},{17,25},{2,10},{10,18},{18,26},{... | collective-permute-start | bytes 8640008 | tf_op jit(solution)/shard_map/ppermute | solution.py:15
  29.9 66.9 %collective-permute-start.3 = (bf16[150,9600]{1,0:T(8,128)(2,1)}, bf16[150,9600]{1,0:T(8,128)(2,1)}, u32[]{:S(2)}, u32[]{:S(2)}) collective-permute-start(bf16[150,9600]{1,0:T(8,128)(2,1)} %bitcast.8), channel_id=1, source_target_pairs={{8,0},{16,8},{24,16},{9,1},{17,9},{25,17},{10,2},{18,10},{26,18},{... | collective-permute-start | bytes 8640008 | tf_op jit(solution)/shard_map/ppermute | solution.py:16
  91.1 93.5 %collective-permute-start.5 = (bf16[150,9600]{1,0:T(8,128)(2,1)}, bf16[150,9600]{1,0:T(8,128)(2,1)}, u32[]{:S(2)}, u32[]{:S(2)}) collective-permute-start(bf16[150,9600]{1,0:T(8,128)(2,1)} %collective-permute-done.1), channel_id=1, source_target_pairs={{8,16},{16,24},{9,17},{17,25},{10,18},{18,26},{11,19},{19,27},{12,... | collective-permute-start | bytes 8640008 | tf_op jit(solution)/shard_map/ppermute | solution.py:15
  93.3 294.1 %all-gather.7.cloned.1.call-start = ((), (), s32[]{:S(2)}) async-start(), calls=%async_computation.2 | async-start | bytes 12976128 | tf_op jit(solution)/shard_map/all_gather | solution.py:26
  93.4 119.3 %collective-permute-start = (bf16[150,9600]{1,0:T(8,128)(2,1)}, bf16[150,9600]{1,0:T(8,128)(2,1)}, u32[]{:S(2)}, u32[]{:S(2)}) collective-permute-start(bf16[150,9600]{1,0:T(8,128)(2,1)} %bitcast.8), channel_id=1, source_target_pairs={{0,4},{4,0},{1,5},{5,1},{2,6},{6,2},{3,7},{7,3},{8,12},{12,8},{9,1... | collective-permute-start | bytes 8640008 | tf_op jit(solution)/shard_map/ppermute | solution.py:46
  96.8 117.2 %collective-permute-start.7 = (bf16[150,9600]{1,0:T(8,128)(2,1)}, bf16[150,9600]{1,0:T(8,128)(2,1)}, u32[]{:S(2)}, u32[]{:S(2)}) collective-permute-start(bf16[150,9600]{1,0:T(8,128)(2,1)} %collective-permute-done.3), channel_id=1, source_target_pairs={{8,0},{16,8},{9,1},{17,9},{10,2},{18,10},{11,3},{19,11},{12,4},{20... | collective-permute-start | bytes 8640008 | tf_op jit(solution)/shard_map/ppermute | solution.py:16
  98.1 513.8 %all-reduce.3.cloned.1.call-start = ((), (), s32[]{:S(2)}) async-start(), calls=%async_computation.3 | async-start | bytes 6144000
  184.0 43.0 %collective-permute-start.2 = (bf16[150,9600]{1,0:T(8,128)(2,1)}, bf16[150,9600]{1,0:T(8,128)(2,1)}, u32[]{:S(2)}, u32[]{:S(2)}) collective-permute-start(bf16[150,9600]{1,0:T(8,128)(2,1)} %collective-permute-done.1), channel_id=1, source_target_pairs={{0,4},{4,0},{1,5},{5,1},{2,6},{6,2},{3,7},{7,3},{8,12},{12,8},{9,1... | collective-permute-start | bytes 8640008 | tf_op jit(solution)/shard_map/ppermute | solution.py:46
  184.0 57.4 %collective-permute-start.4 = (bf16[150,9600]{1,0:T(8,128)(2,1)}, bf16[150,9600]{1,0:T(8,128)(2,1)}, u32[]{:S(2)}, u32[]{:S(2)}) collective-permute-start(bf16[150,9600]{1,0:T(8,128)(2,1)} %collective-permute-done.3), channel_id=1, source_target_pairs={{0,4},{4,0},{1,5},{5,1},{2,6},{6,2},{3,7},{7,3},{8,12},{12,8},{9,1... | collective-permute-start | bytes 8640008 | tf_op jit(solution)/shard_map/ppermute | solution.py:46
  184.5 163.4 %collective-permute-start.6 = (bf16[150,9600]{1,0:T(8,128)(2,1)}, bf16[150,9600]{1,0:T(8,128)(2,1)}, u32[]{:S(2)}, u32[]{:S(2)}) collective-permute-start(bf16[150,9600]{1,0:T(8,128)(2,1)} %collective-permute-done.5), channel_id=1, source_target_pairs={{0,4},{4,0},{1,5},{5,1},{2,6},{6,2},{3,7},{7,3},{8,12},{12,8},{9,1... | collective-permute-start | bytes 8640008 | tf_op jit(solution)/shard_map/ppermute | solution.py:46
  205.0 9.4 %copy-start = (bf16[600,9600]{1,0:T(8,128)(2,1)S(1)}, bf16[600,9600]{1,0:T(8,128)(2,1)}, u32[]{:S(2)}) copy-start(bf16[600,9600]{1,0:T(8,128)(2,1)} %reshape.21) | copy-start | bytes 34560004
  212.6 41.4 %collective-permute-start.9 = (bf16[150,9600]{1,0:T(8,128)(2,1)}, bf16[150,9600]{1,0:T(8,128)(2,1)S(1)}, u32[]{:S(2)}, u32[]{:S(2)}) collective-permute-start(bf16[150,9600]{1,0:T(8,128)(2,1)} %collective-permute-done.5), channel_id=1, source_target_pairs={{16,24},{17,25},{18,26},{19,27},{20,28},{21,29},{22,30},{23,31}} | collective-permute-start | bytes 8640008 | tf_op jit(solution)/shard_map/ppermute | solution.py:15
  213.9 146.7 %collective-permute-start.8 = (bf16[150,9600]{1,0:T(8,128)(2,1)}, bf16[150,9600]{1,0:T(8,128)(2,1)S(1)}, u32[]{:S(2)}, u32[]{:S(2)}) collective-permute-start(bf16[150,9600]{1,0:T(8,128)(2,1)} %collective-permute-done.7), channel_id=1, source_target_pairs={{0,4},{4,0},{1,5},{5,1},{2,6},{6,2},{3,7},{7,3},{8,12},{12,8},{9,1... | collective-permute-start | bytes 8640008 | tf_op jit(solution)/shard_map/ppermute | solution.py:46
  227.0 120.8 %collective-permute-start.11 = (bf16[150,9600]{1,0:T(8,128)(2,1)}, bf16[150,9600]{1,0:T(8,128)(2,1)S(1)}, u32[]{:S(2)}, u32[]{:S(2)}) collective-permute-start(bf16[150,9600]{1,0:T(8,128)(2,1)} %collective-permute-done.7), channel_id=1, source_target_pairs={{8,0},{9,1},{10,2},{11,3},{12,4},{13,5},{14,6},{15,7}} | collective-permute-start | bytes 8640008 | tf_op jit(solution)/shard_map/ppermute | solution.py:16
  254.1 115.4 %collective-permute-start.10 = (bf16[150,9600]{1,0:T(8,128)(2,1)S(1)}, bf16[150,9600]{1,0:T(8,128)(2,1)S(1)}, u32[]{:S(2)}, u32[]{:S(2)}) collective-permute-start(bf16[150,9600]{1,0:T(8,128)(2,1)S(1)} %collective-permute-done.9), channel_id=1, source_target_pairs={{0,4},{4,0},{1,5},{5,1},{2,6},{6,2},{3,7},{7,3},{8,12},{12,8},{9,1... | collective-permute-start | bytes 8640008 | tf_op jit(solution)/shard_map/ppermute | solution.py:46
  347.9 30.6 %collective-permute-start.12 = (bf16[150,9600]{1,0:T(8,128)(2,1)S(1)}, bf16[150,9600]{1,0:T(8,128)(2,1)S(1)}, u32[]{:S(2)}, u32[]{:S(2)}) collective-permute-start(bf16[150,9600]{1,0:T(8,128)(2,1)S(1)} %collective-permute-done.11), channel_id=1, source_target_pairs={{0,4},{4,0},{1,5},{5,1},{2,6},{6,2},{3,7},{7,3},{8,12},{12,8},{9,1... | collective-permute-start | bytes 8640008 | tf_op jit(solution)/shard_map/ppermute | solution.py:46
  520.5 5.1 copy-start.1
Sparse Core Ops, SparseCore 0:
  93.4 86.0 all-gather.4
  181.2 131.2 all-gather.6
  525.7 86.1 all-reduce.2

commit v3 on v2

--- a/solution.py
+++ b/solution.py
@@ -22,13 +22,24 @@
 def ladder_term(amplitudes, factors, nvirt):
     nj = amplitudes.shape[1]
     t = lax.all_gather(amplitudes[0], "orb", axis=0, tiled=False)
-    tm = t.transpose(0, 2, 1, 3).reshape(nvirt, nj * nvirt)
-    g = lax.all_gather(factors, PAIR, axis=0, tiled=False)
-    nq = factors.shape[0]
-    cube = g.transpose(1, 0, 2).reshape(nq, nvirt, nvirt)
-    inner = jnp.einsum("qac,cn->qan", cube, tm, preferred_element_type=jnp.float32).astype(jnp.bfloat16)
-    inner = inner.reshape(nq, nvirt, nj, nvirt)
-    return jnp.einsum("qajd,qbd->ajb", inner, cube, preferred_element_type=jnp.float32)
+    nq, cols = factors.shape
+    if cols % nvirt == 0:
+        g = lax.all_gather(factors.reshape(nq, cols // nvirt, nvirt), PAIR, axis=0, tiled=False)
+        cube = None
+    else:
+        g = lax.all_gather(factors, PAIR, axis=0, tiled=False)
+        cube = g.transpose(1, 0, 2).reshape(nq, nvirt, nvirt)
+    parts = []
+    for j in range(nj):
+        tj = t[:, j].reshape(nvirt, nvirt)
+        if cube is None:
+            inner = jnp.einsum("pqac,cd->pqad", g, tj, preferred_element_type=jnp.float32).astype(jnp.bfloat16)
+            lj = jnp.einsum("pqad,rqbd->parb", inner, g, preferred_element_type=jnp.float32)
+        else:
+            inner = jnp.einsum("qac,cd->qad", cube, tj, preferred_element_type=jnp.float32).astype(jnp.bfloat16)
+            lj = jnp.einsum("qad,qbd->ab", inner, cube, preferred_element_type=jnp.float32)
+        parts.append(lj.reshape(nvirt, nvirt))
+    return jnp.stack(parts, axis=1)
 
 
 def crossed_term(crossed_amplitudes, crossed_coupling, nvirt, norb, nchip):
@@ -59,7 +70,23 @@
     ladder = ladder_term(amplitudes, factors, nvirt)
     crossed = crossed_term(crossed_amplitudes, crossed_coupling, nvirt, norb, nchip)
     total = (ladder + crossed).reshape((norb, nvirt // norb) + ladder.shape[1:])
-    return lax.psum_scatter(total, "orb", scatter_dimension=0, tiled=True)
+    return reduce_scatter(total, norb)[None]
+
+
+def reduce_scatter(total, norb):
+    me = lax.axis_index("orb")
+    acc = lax.dynamic_index_in_dim(total, me, axis=0, keepdims=False)
+    pow2 = norb & (norb - 1) == 0
+    for s in range(1, norb):
+        if pow2:
+            pairs = [(o, o ^ s) for o in range(norb)]
+            dest = jnp.bitwise_xor(me, s)
+        else:
+            pairs = [(o, (o + s) % norb) for o in range(norb)]
+            dest = (me + s) % norb
+        blk = lax.dynamic_index_in_dim(total, dest, axis=0, keepdims=False)
+        acc = acc + lax.ppermute(blk, "orb", pairs)
+    return acc
 
 
 def solution(mesh):

time: 629 us -> 502 us (0.80)
  waiting for transfers between devices: 324 us -> 245 us
  local copies, waits for them, and re-layouts: 138 us -> 70.5 us
  matrix products: 123 us -> 137 us
    reshape x5 -> x0, local copies, waits for them, and re-layouts: 87 us -> none  [the longest x1 40.1 us: ladder_term(): inner = inner.reshape(nq, nvirt, nj, nvirt)]
    unnamed x4 -> x2, waiting for transfers between devices: 85.7 us -> 0.03 us
    ppermute x0 -> x3, waiting for transfers between devices: none -> 32.7 us  [reduce_scatter(): acc = acc + lax.ppermute(blk, 'orb', pairs)]
    ppermute x3, waiting for transfers between devices: 97 us -> 73.9 us  [relay(): left = lax.ppermute(left, 'zz', [(j, j - 1) for j in range(1, n - s + 1)])]
    transpose x1 -> x0, local copies, waits for them, and re-layouts: 12.4 us -> none  [ladder_term(): cube = g.transpose(1, 0, 2).reshape(nq, nvirt, nvirt)]
    another operation x0 -> x5, local copies, waits for them, and re-layouts: none -> 10.1 us  [the longest x2 4.65 us: ladder_term(): return jnp.stack(parts, axis=1)]
    slice x0 -> x1, local copies, waits for them, and re-layouts: none -> 9.63 us  [ladder_term(): tj = t[:, j].reshape(nvirt, nvirt)]
    dot_general x14, matrix products: 80.2 us -> 89.6 us  [crossed_term(): part = jnp.einsum('ak,nk->an', lhs, b, preferred_element_type=jnp.float32)]
  transfers between devices with their start and end apart: 17 -> 19, of which waited for: 5 -> 6; matrix products, arithmetic and copies ran while one was open for 18% -> 28% of each run, Pallas kernels for 0% -> 0%
where the time goes in v3:
time: 502 us; the launch traced here: 497 us
  waiting for transfers between devices  245 us (49%)
  matrix products  137 us (27%)
  local copies, waits for them, and re-layouts  70.5 us (14%)
  starting transfers between devices  25.1 us (5%)
  between operations  14 us (3%)
    dot_general x14, matrix products, crossed_term(): part = jnp.einsum('ak,nk->an', lhs, b, preferred_element_type=jnp.float32)  89.6 us
    all_gather x1, waiting for transfers between devices, ladder_term(): t = lax.all_gather(amplitudes[0], 'orb', axis=0, tiled=False)  78.4 us
    ppermute x3, waiting for transfers between devices, relay(): left = lax.ppermute(left, 'zz', [(j, j - 1) for j in range(1, n - s + 1)])  73.9 us
    ppermute x3, waiting for transfers between devices, relay(): right = lax.ppermute(right, 'zz', [(i, i + 1) for i in range(s - 1, n - 1)])  59.9 us
    ppermute x3, waiting for transfers between devices, reduce_scatter(): acc = acc + lax.ppermute(blk, 'orb', pairs)  32.7 us
    dot_general x2, matrix products, ladder_term(): jnp.einsum('pqac,cd->pqad', g, tj, preferred_element_type=jnp.float32)  24 us
    dot_general x2, matrix products, ladder_term(): jnp.einsum('pqad,rqbd->parb', inner, g, preferred_element_type=jnp.float32)  23.9 us
    reshape x1, local copies, waits for them, and re-layouts, crossed_term(): lhs = r.transpose(0, 2, 1, 3).reshape(norb * nva, kl * nvirt)  20.1 us
  transfers between devices with their start and end apart: 19, of which 6 were waited for; matrix products, arithmetic and copies ran while one was open for 28% of the time, Pallas kernels for 0%

profile of v3, /device:TPU:0, one launch (start us, length us, event | category | flops | bytes accessed | tf_op | source)
XLA Modules:
  0.0 496.9 jit_solution(11940839149197209218)
XLA Ops:
  6.5 10.4 %copy.22 = bf16[4,16,150,600]{3,1,2,0:T(8,128)(2,1)} copy(bf16[4,16,150,600]{3,1,0,2:T(8,128)(2,1)} %bitcast.156) | data formatting | bytes 23040000 | tf_op jit(solution)/shard_map/reshape;squeeze | solution.py:49
  17.0 6.5 %all-to-all-start = ((bf16[4,16,150,600]{3,1,2,0:T(8,128)(2,1)}), bf16[4,16,150,600]{3,1,2,0:T(8,128)(2,1)}, u32[]{:S(2)}, u32[]{:S(2)}) async-start(bf16[4,16,150,600]{3,1,2,0:T(8,128)(2,1)} %copy.22), calls=%async_computation | async-start | bytes 24576000 | tf_op jit(solution)/shard_map/all_to_all | solution.py:50
  23.5 6.6 %collective-permute-start.1 = (bf16[150,9600]{1,0:T(8,128)(2,1)}, bf16[150,9600]{1,0:T(8,128)(2,1)}, u32[]{:S(2)}, u32[]{:S(2)}) collective-permute-start(bf16[150,9600]{1,0:T(8,128)(2,1)} %bitcast.157), channel_id=1, source_target_pairs={{0,8},{8,16},{16,24},{1,9},{9,17},{17,25},{2,10},{10,18},{18,26},{... | collective-permute-start | bytes 8640008 | tf_op jit(solution)/shard_map/ppermute | solution.py:15
  30.1 1.3 collective-permute-start.3
  31.4 59.9 %collective-permute-done.1 = bf16[150,9600]{1,0:T(8,128)(2,1)} collective-permute-done((bf16[150,9600]{1,0:T(8,128)(2,1)}, bf16[150,9600]{1,0:T(8,128)(2,1)}, u32[]{:S(2)}, u32[]{:S(2)}) %collective-permute-start.1) | collective-permute-done | bytes 2880032 | tf_op jit(solution)/shard_map/ppermute | solution.py:15
  91.3 2.3 collective-permute-start.5
  93.8 3.2 collective-permute-done.3
  97.0 1.3 collective-permute-start.7
  98.3 3.0 all_gather_reshape.3
  101.3 78.4 %all-gather.5.cloned.1.call-done = bf16[4,2,150,600]{3,1,2,0:T(2,128)(2,1)} async-done(((bf16[1,2,150,600]{3,1,2,0:T(2,128)(2,1)}), bf16[4,2,150,600]{3,1,2,0:T(2,128)(2,1)}) %all-gather.5.cloned.1.call-update) | async-done | bytes 1440016 | tf_op jit(solution)/shard_map/all_gather | solution.py:24
  179.7 9.6 %slice_reduce_fusion.1 = (bf16[4,150,600]{2,1,0:T(8,128)(2,1)S(1)}, bf16[4,150,600]{2,1,0:T(8,128)(2,1)S(1)}) fusion(bf16[4,2,150,600]{3,1,2,0:T(2,128)(2,1)} %all-gather.5.cloned.1.call-done), kind=kLoop, calls=%fused_computation.14 | loop fusion | bytes 2880000 | tf_op jit(solution)/shard_map/slice | solution.py:34
  189.4 1.2 reshape.14
  192.3 20.1 %reshape.12 = bf16[600,9600]{1,0:T(8,128)(2,1)} reshape(bf16[4,150,16,600]{3,2,1,0:T(8,128)(2,1)} %bitcast.12) | data formatting | bytes 23040000 | tf_op jit(solution)/shard_map/reshape | solution.py:51
  212.6 1.6 copy-done.5
  214.2 8.7 %fusion.22 = f32[600,8,150]{0,2,1:T(8,128)S(1)} fusion(f32[600,8,150]{0,2,1:T(8,128)S(1)} %broadcast_in_dim.48, s32[]{:T(128)S(6)} %select_n.68, bf16[600,9600]{1,0:T(8,128)(2,1)} %reshape.12, bf16[9600,150]{0,1:T(8,128)(2,1)S(1)} %copy-done.5), kind=kOutput, calls=%fused_computation.29 | convolution fusion | flops 1728000000 | bytes 14827524 | tf_op jit(solution)/shard_map/ak,nk->an/dot_general | solution.py:59
  224.5 6.2 %fusion.24 = f32[600,8,150]{0,2,1:T(8,128)S(1)} fusion(f32[600,8,150]{0,2,1:T(8,128)S(1)} %fusion.22, s32[]{:T(128)S(6)} %select_n.69, bf16[600,9600]{1,0:T(8,128)(2,1)S(1)} %copy-done, bf16[150,9600]{1,0:T(8,128)(2,1)} %collective-permute-done), kind=kOutput, calls=%fused_computation.31 | convolution fusion | flops 1728089984 | bytes 15178244 | tf_op jit(solution)/shard_map/ak,nk->an/dot_general | solution.py:59
  230.8 6.3 %add_dynamic-update-slice_fusion.8 = f32[600,8,150]{0,2,1:T(8,128)S(1)} fusion(f32[600,8,150]{0,2,1:T(8,128)S(1)} %fusion.24, s32[]{:T(128)S(6)} %select_n.70, bf16[600,9600]{1,0:T(8,128)(2,1)S(1)} %copy-done, bf16[150,9600]{1,0:T(8,128)(2,1)} %collective-permute-done.1), kind=kOutput, calls=%fused_computation.55 | convolution fusion | flops 1728089984 | bytes 15178244 | tf_op jit(solution)/shard_map/ak,nk->an/dot_general | solution.py:59
  237.0 1.3 collective-permute-start.11
  238.3 6.2 %fusion.26 = f32[600,8,150]{0,2,1:T(8,128)S(1)} fusion(f32[600,8,150]{0,2,1:T(8,128)S(1)} %add_dynamic-update-slice_fusion.8, s32[]{:T(128)S(6)} %select_n.71, bf16[600,9600]{1,0:T(8,128)(2,1)S(1)} %copy-done, bf16[150,9600]{1,0:T(8,128)(2,1)} %collective-permute-done.2), kind=kOutput, calls=%fused_computation.33 | convolution fusion | flops 1728089984 | bytes 15178244 | tf_op jit(solution)/shard_map/ak,nk->an/dot_general | solution.py:59
  244.6 6.3 %add_dynamic-update-slice_fusion.7 = f32[600,8,150]{0,2,1:T(8,128)S(1)} fusion(f32[600,8,150]{0,2,1:T(8,128)S(1)} %fusion.26, s32[]{:T(128)S(6)} %select_n.72, bf16[600,9600]{1,0:T(8,128)(2,1)S(1)} %copy-done, bf16[150,9600]{1,0:T(8,128)(2,1)} %collective-permute-done.3), kind=kOutput, calls=%fused_computation.54 | convolution fusion | flops 1728089984 | bytes 15178244 | tf_op jit(solution)/shard_map/ak,nk->an/dot_general | solution.py:59
  250.8 6.2 %add_dynamic-update-slice_fusion.6 = f32[600,8,150]{0,2,1:T(8,128)S(1)} fusion(f32[600,8,150]{0,2,1:T(8,128)S(1)} %add_dynamic-update-slice_fusion.7, s32[]{:T(128)S(6)} %select_n.73, bf16[600,9600]{1,0:T(8,128)(2,1)S(1)} %copy-done, bf16[150,9600]{1,0:T(8,128)(2,1)} %collective-permute-done.4), kind=kOutput, calls=%fused_computation.53 | convolution fusion | flops 1728089984 | bytes 15178244 | tf_op jit(solution)/shard_map/ak,nk->an/dot_general | solution.py:59
  257.1 6.2 %add_dynamic-update-slice_fusion.5 = f32[600,8,150]{0,2,1:T(8,128)S(1)} fusion(f32[600,8,150]{0,2,1:T(8,128)S(1)} %add_dynamic-update-slice_fusion.6, s32[]{:T(128)S(6)} %select_n.74, bf16[600,9600]{1,0:T(8,128)(2,1)S(1)} %copy-done, bf16[150,9600]{1,0:T(8,128)(2,1)} %collective-permute-done.5), kind=kOutput, calls=%fused_computation.52 | convolution fusion | flops 1728089984 | bytes 15178244 | tf_op jit(solution)/shard_map/ak,nk->an/dot_general | solution.py:59
  263.5 70.6 %collective-permute-done.11 = bf16[150,9600]{1,0:T(8,128)(2,1)S(1)} collective-permute-done((bf16[150,9600]{1,0:T(8,128)(2,1)}, bf16[150,9600]{1,0:T(8,128)(2,1)S(1)}, u32[]{:S(2)}, u32[]{:S(2)}) %collective-permute-start.11) | collective-permute-done | bytes 2880032 | tf_op jit(solution)/shard_map/ppermute | solution.py:16
  334.1 15.0 %fusion.28 = f32[600,8,150]{0,2,1:T(8,128)S(1)} fusion(f32[600,8,150]{0,2,1:T(8,128)S(1)} %add_dynamic-update-slice_fusion.5, s32[]{:T(128)S(6)} %select_n.75, bf16[600,9600]{1,0:T(8,128)(2,1)S(1)} %copy-done, bf16[150,9600]{1,0:T(8,128)(2,1)} %collective-permute-done.6), kind=kOutput, calls=%fused_computation.35 | convolution fusion | flops 1728089984 | bytes 15178244 | tf_op jit(solution)/shard_map/ak,nk->an/dot_general | solution.py:59
  349.1 6.2 %add_dynamic-update-slice_fusion.4 = f32[600,8,150]{0,2,1:T(8,128)S(1)} fusion(f32[600,8,150]{0,2,1:T(8,128)S(1)} %fusion.28, s32[]{:T(128)S(6)} %select_n.76, bf16[600,9600]{1,0:T(8,128)(2,1)S(1)} %copy-done, bf16[150,9600]{1,0:T(8,128)(2,1)} %collective-permute-done.7), kind=kOutput, calls=%fused_computation.51 | convolution fusion | flops 1728089984 | bytes 15178244 | tf_op jit(solution)/shard_map/ak,nk->an/dot_general | solution.py:59
  355.4 4.4 add_dynamic-update-slice_fusion.3
  359.8 4.4 add_dynamic-update-slice_fusion.2
  364.2 4.6 fusion.30
  368.8 4.4 add_dynamic-update-slice_fusion.1
  373.2 4.4 add_dynamic-update-slice_fusion
  377.6 5.5 %reshape.23 = f32[4,150,2,600]{1,0,3,2:T(4,128)} reshape(f32[600,8,150]{0,2,1:T(8,128)S(1)} %add_dynamic-update-slice_fusion) | data formatting | bytes 5760000 | tf_op jit(solution)/shard_map/reshape | solution.py:63
  383.1 6.2 %copy.24 = f32[4,150,2,600]{3,1,0,2:T(8,128)} copy(f32[4,150,2,600]{1,0,3,2:T(4,128)} %reshape.23) | data formatting | bytes 5760000 | tf_op jit(solution)/shard_map/reshape | solution.py:63
  389.4 12.5 %fusion.77 = bf16[8,12,75,600,1]{3,2,1,4,0:T(8,128)(2,1)S(1)} fusion(bf16[8,12,75,600]{3,2,1,0:T(8,128)(2,1)} %all-gather.3.cloned.1.call-done, bf16[600,600,1,1]{1,0,2,3:T(8,128)(2,1)S(1)} %copy-done.3), kind=kOutput, calls=%fused_computation.3.clone.clone.clone.1 | convolution fusion | flops 5188320256 | bytes 18000000 | tf_op jit(solution)/shard_map/pqac,cd->pqad/dot_general | solution.py:36
  401.9 10.7 %fusion.12 = f32[8,75,8,75]{3,1,2,0:T(8,128)S(1)} fusion(bf16[8,12,75,600]{3,2,1,0:T(8,128)(2,1)S(1)} %copy-done.4, bf16[8,12,75,600,1]{3,2,1,4,0:T(8,128)(2,1)S(1)} %fusion.77), kind=kOutput, calls=%fused_computation.11 | convolution fusion | flops 5184000000 | bytes 18720000 | tf_op jit(solution)/shard_map/pqad,rqbd->parb/dot_general | solution.py:37
  413.4 2.3 stack.7
  415.7 11.5 %fusion.81 = bf16[8,12,75,600,1]{3,2,1,4,0:T(8,128)(2,1)S(1)} fusion(bf16[8,12,75,600]{3,2,1,0:T(8,128)(2,1)} %all-gather.3.cloned.1.call-done, bf16[600,600,1,1]{1,0,2,3:T(8,128)(2,1)S(1)} %copy-done.2), kind=kOutput, calls=%fused_computation.1.clone.clone.clone | convolution fusion | flops 5188320256 | bytes 18000000 | tf_op jit(solution)/shard_map/pqac,cd->pqad/dot_general | solution.py:36
  427.2 13.2 %fusion.17 = f32[8,75,8,75]{3,1,2,0:T(8,128)S(1)} fusion(bf16[8,12,75,600]{3,2,1,0:T(8,128)(2,1)} %all-gather.3.cloned.1.call-done, bf16[8,12,75,600,1]{3,2,1,4,0:T(8,128)(2,1)S(1)} %fusion.81), kind=kOutput, calls=%fused_computation.12 | convolution fusion | flops 5184000000 | bytes 18720000 | tf_op jit(solution)/shard_map/pqad,rqbd->parb/dot_general | solution.py:37
  441.1 2.4 stack.8
  443.5 3.1 maximum_add_fusion
  446.8 1.3 copy.25
  448.0 1.5 collective-permute-start.13
  449.5 1.3 copy.27
  450.8 1.5 collective-permute-start.14
  452.3 1.3 copy.29
  454.1 14.3 %collective-permute-done.13 = f32[150,2,600]{2,1,0:T(2,128)} collective-permute-done((f32[150,2,600]{2,1,0:T(2,128)}, f32[150,2,600]{2,1,0:T(2,128)}, u32[]{:S(2)}, u32[]{:S(2)}) %collective-permute-start.13) | collective-permute-done | bytes 720032 | tf_op jit(solution)/shard_map/ppermute | solution.py:88
  468.4 18.4 %collective-permute-done.14 = f32[150,2,600]{2,1,0:T(2,128)} collective-permute-done((f32[150,2,600]{2,1,0:T(2,128)}, f32[150,2,600]{2,1,0:T(2,128)}, u32[]{:S(2)}, u32[]{:S(2)}) %collective-permute-start.14) | collective-permute-done | bytes 720032 | tf_op jit(solution)/shard_map/ppermute | solution.py:88
  486.8 1.8 fusion.33
  488.6 1.3 copy.31
  (42 shorter events, 6.1 us)
Async XLA Ops:
  17.0 81.3 %copy-start.1 = (bf16[12,45000]{1,0:T(8,128)(2,1)S(1)}, bf16[12,45000]{1,0:T(8,128)(2,1)}, u32[]{:S(2)}) copy-start(bf16[12,45000]{1,0:T(8,128)(2,1)} %param.5) | copy-start | bytes 3240004
  17.0 175.4 %all-to-all-start = ((bf16[4,16,150,600]{3,1,2,0:T(8,128)(2,1)}), bf16[4,16,150,600]{3,1,2,0:T(8,128)(2,1)}, u32[]{:S(2)}, u32[]{:S(2)}) async-start(bf16[4,16,150,600]{3,1,2,0:T(8,128)(2,1)} %copy.22), calls=%async_computation | async-start | bytes 24576000 | tf_op jit(solution)/shard_map/all_to_all | solution.py:50
  23.5 156.3 %all-gather.5.cloned.1.call-start = ((), (), s32[]{:S(2)}) async-start(), calls=%async_computation.2 | async-start | bytes 1920000 | tf_op jit(solution)/shard_map/all_gather | solution.py:24
  23.5 67.8 %collective-permute-start.1 = (bf16[150,9600]{1,0:T(8,128)(2,1)}, bf16[150,9600]{1,0:T(8,128)(2,1)}, u32[]{:S(2)}, u32[]{:S(2)}) collective-permute-start(bf16[150,9600]{1,0:T(8,128)(2,1)} %bitcast.157), channel_id=1, source_target_pairs={{0,8},{8,16},{16,24},{1,9},{9,17},{17,25},{2,10},{10,18},{18,26},{... | collective-permute-start | bytes 8640008 | tf_op jit(solution)/shard_map/ppermute | solution.py:15
  30.1 66.9 %collective-permute-start.3 = (bf16[150,9600]{1,0:T(8,128)(2,1)}, bf16[150,9600]{1,0:T(8,128)(2,1)}, u32[]{:S(2)}, u32[]{:S(2)}) collective-permute-start(bf16[150,9600]{1,0:T(8,128)(2,1)} %bitcast.158), channel_id=1, source_target_pairs={{8,0},{16,8},{24,16},{9,1},{17,9},{25,17},{10,2},{18,10},{26,18},{... | collective-permute-start | bytes 8640008 | tf_op jit(solution)/shard_map/ppermute | solution.py:16
  91.3 101.1 %collective-permute-start.5 = (bf16[150,9600]{1,0:T(8,128)(2,1)}, bf16[150,9600]{1,0:T(8,128)(2,1)}, u32[]{:S(2)}, u32[]{:S(2)}) collective-permute-start(bf16[150,9600]{1,0:T(8,128)(2,1)} %collective-permute-done.1), channel_id=1, source_target_pairs={{8,16},{16,24},{9,17},{17,25},{10,18},{18,26},{11,19},{19,27},{12,... | collective-permute-start | bytes 8640008 | tf_op jit(solution)/shard_map/ppermute | solution.py:15
  93.6 295.7 %all-gather.3.cloned.1.call-start = ((), (), s32[]{:S(2)}) async-start(), calls=%async_computation.1 | async-start | bytes 11059200 | tf_op jit(solution)/shard_map/all_gather | solution.py:27
  93.7 129.2 %collective-permute-start = (bf16[150,9600]{1,0:T(8,128)(2,1)}, bf16[150,9600]{1,0:T(8,128)(2,1)}, u32[]{:S(2)}, u32[]{:S(2)}) collective-permute-start(bf16[150,9600]{1,0:T(8,128)(2,1)} %bitcast.159), channel_id=1, source_target_pairs={{0,4},{4,0},{1,5},{5,1},{2,6},{6,2},{3,7},{7,3},{8,12},{12,8},{9,1... | collective-permute-start | bytes 8640008 | tf_op jit(solution)/shard_map/ppermute | solution.py:57
  97.0 127.0 %collective-permute-start.7 = (bf16[150,9600]{1,0:T(8,128)(2,1)}, bf16[150,9600]{1,0:T(8,128)(2,1)}, u32[]{:S(2)}, u32[]{:S(2)}) collective-permute-start(bf16[150,9600]{1,0:T(8,128)(2,1)} %collective-permute-done.3), channel_id=1, source_target_pairs={{8,0},{16,8},{9,1},{17,9},{10,2},{18,10},{11,3},{19,11},{12,4},{20... | collective-permute-start | bytes 8640008 | tf_op jit(solution)/shard_map/ppermute | solution.py:16
  191.8 45.2 %collective-permute-start.2 = (bf16[150,9600]{1,0:T(8,128)(2,1)}, bf16[150,9600]{1,0:T(8,128)(2,1)}, u32[]{:S(2)}, u32[]{:S(2)}) collective-permute-start(bf16[150,9600]{1,0:T(8,128)(2,1)} %collective-permute-done.1), channel_id=1, source_target_pairs={{0,4},{4,0},{1,5},{5,1},{2,6},{6,2},{3,7},{7,3},{8,12},{12,8},{9,1... | collective-permute-start | bytes 8640008 | tf_op jit(solution)/shard_map/ppermute | solution.py:57
  191.8 59.0 %collective-permute-start.4 = (bf16[150,9600]{1,0:T(8,128)(2,1)}, bf16[150,9600]{1,0:T(8,128)(2,1)}, u32[]{:S(2)}, u32[]{:S(2)}) collective-permute-start(bf16[150,9600]{1,0:T(8,128)(2,1)} %collective-permute-done.3), channel_id=1, source_target_pairs={{0,4},{4,0},{1,5},{5,1},{2,6},{6,2},{3,7},{7,3},{8,12},{12,8},{9,1... | collective-permute-start | bytes 8640008 | tf_op jit(solution)/shard_map/ppermute | solution.py:57
  192.3 141.8 %collective-permute-start.6 = (bf16[150,9600]{1,0:T(8,128)(2,1)}, bf16[150,9600]{1,0:T(8,128)(2,1)}, u32[]{:S(2)}, u32[]{:S(2)}) collective-permute-start(bf16[150,9600]{1,0:T(8,128)(2,1)} %collective-permute-done.5), channel_id=1, source_target_pairs={{0,4},{4,0},{1,5},{5,1},{2,6},{6,2},{3,7},{7,3},{8,12},{12,8},{9,1... | collective-permute-start | bytes 8640008 | tf_op jit(solution)/shard_map/ppermute | solution.py:57
  212.4 1.8 copy-start.5
  214.2 10.3 %copy-start = (bf16[600,9600]{1,0:T(8,128)(2,1)S(1)}, bf16[600,9600]{1,0:T(8,128)(2,1)}, u32[]{:S(2)}) copy-start(bf16[600,9600]{1,0:T(8,128)(2,1)} %reshape.12) | copy-start | bytes 34560004
  222.9 40.4 %collective-permute-start.9 = (bf16[150,9600]{1,0:T(8,128)(2,1)}, bf16[150,9600]{1,0:T(8,128)(2,1)S(1)}, u32[]{:S(2)}, u32[]{:S(2)}) collective-permute-start(bf16[150,9600]{1,0:T(8,128)(2,1)} %collective-permute-done.5), channel_id=1, source_target_pairs={{16,24},{17,25},{18,26},{19,27},{20,28},{21,29},{22,30},{23,31}} | collective-permute-start | bytes 8640008 | tf_op jit(solution)/shard_map/ppermute | solution.py:15
  224.0 131.3 %collective-permute-start.8 = (bf16[150,9600]{1,0:T(8,128)(2,1)}, bf16[150,9600]{1,0:T(8,128)(2,1)S(1)}, u32[]{:S(2)}, u32[]{:S(2)}) collective-permute-start(bf16[150,9600]{1,0:T(8,128)(2,1)} %collective-permute-done.7), channel_id=1, source_target_pairs={{0,4},{4,0},{1,5},{5,1},{2,6},{6,2},{3,7},{7,3},{8,12},{12,8},{9,1... | collective-permute-start | bytes 8640008 | tf_op jit(solution)/shard_map/ppermute | solution.py:57
  237.0 97.1 %collective-permute-start.11 = (bf16[150,9600]{1,0:T(8,128)(2,1)}, bf16[150,9600]{1,0:T(8,128)(2,1)S(1)}, u32[]{:S(2)}, u32[]{:S(2)}) collective-permute-start(bf16[150,9600]{1,0:T(8,128)(2,1)} %collective-permute-done.7), channel_id=1, source_target_pairs={{8,0},{9,1},{10,2},{11,3},{12,4},{13,5},{14,6},{15,7}} | collective-permute-start | bytes 8640008 | tf_op jit(solution)/shard_map/ppermute | solution.py:16
  263.3 100.8 %collective-permute-start.10 = (bf16[150,9600]{1,0:T(8,128)(2,1)S(1)}, bf16[150,9600]{1,0:T(8,128)(2,1)S(1)}, u32[]{:S(2)}, u32[]{:S(2)}) collective-permute-start(bf16[150,9600]{1,0:T(8,128)(2,1)S(1)} %collective-permute-done.9), channel_id=1, source_target_pairs={{0,4},{4,0},{1,5},{5,1},{2,6},{6,2},{3,7},{7,3},{8,12},{12,8},{9,1... | collective-permute-start | bytes 8640008 | tf_op jit(solution)/shard_map/ppermute | solution.py:57
  334.1 39.1 %collective-permute-start.12 = (bf16[150,9600]{1,0:T(8,128)(2,1)S(1)}, bf16[150,9600]{1,0:T(8,128)(2,1)S(1)}, u32[]{:S(2)}, u32[]{:S(2)}) collective-permute-start(bf16[150,9600]{1,0:T(8,128)(2,1)S(1)} %collective-permute-done.11), channel_id=1, source_target_pairs={{0,4},{4,0},{1,5},{5,1},{2,6},{6,2},{3,7},{7,3},{8,12},{12,8},{9,1... | collective-permute-start | bytes 8640008 | tf_op jit(solution)/shard_map/ppermute | solution.py:57
  383.1 6.2 %copy-start.3 = (bf16[600,600,1,1]{1,0,2,3:T(8,128)(2,1)S(1)}, bf16[600,600,1,1]{1,0,2,3:T(8,128)(2,1)}, u32[]{:S(2)}) copy-start(bf16[600,600,1,1]{1,0,2,3:T(8,128)(2,1)} %reshape.14) | copy-start | bytes 2160004
  389.4 12.5 %copy-start.4 = (bf16[8,12,75,600]{3,2,1,0:T(8,128)(2,1)S(1)}, bf16[8,12,75,600]{3,2,1,0:T(8,128)(2,1)}, u32[]{:S(2)}) copy-start(bf16[8,12,75,600]{3,2,1,0:T(8,128)(2,1)} %all-gather.3.cloned.1.call-done) | copy-start | bytes 25920004
  413.4 2.3 copy-start.2
  448.0 20.3 %collective-permute-start.13 = (f32[150,2,600]{2,1,0:T(2,128)}, f32[150,2,600]{2,1,0:T(2,128)}, u32[]{:S(2)}, u32[]{:S(2)}) collective-permute-start(f32[150,2,600]{2,1,0:T(2,128)} %copy.25), channel_id=1, source_target_pairs={{0,1},{1,0},{2,3},{3,2},{4,5},{5,4},{6,7},{7,6},{8,9},{9,8},{10,11... | collective-permute-start | bytes 2160008 | tf_op jit(solution)/shard_map/ppermute | solution.py:88
  450.8 36.0 %collective-permute-start.14 = (f32[150,2,600]{2,1,0:T(2,128)}, f32[150,2,600]{2,1,0:T(2,128)}, u32[]{:S(2)}, u32[]{:S(2)}) collective-permute-start(f32[150,2,600]{2,1,0:T(2,128)} %copy.27), channel_id=1, source_target_pairs={{0,2},{1,3},{2,0},{3,1},{4,6},{5,7},{6,4},{7,5},{8,10},{9,11},{10,... | collective-permute-start | bytes 2160008 | tf_op jit(solution)/shard_map/ppermute | solution.py:88
  453.5 33.3 %collective-permute-start.15 = (f32[150,2,600]{2,1,0:T(2,128)}, f32[150,2,600]{2,1,0:T(2,128)}, u32[]{:S(2)}, u32[]{:S(2)}) collective-permute-start(f32[150,2,600]{2,1,0:T(2,128)} %copy.29), channel_id=1, source_target_pairs={{0,3},{1,2},{2,1},{3,0},{4,7},{5,6},{6,5},{7,4},{8,11},{9,10},{10,... | collective-permute-start | bytes 2160008 | tf_op jit(solution)/shard_map/ppermute | solution.py:88
Sparse Core Ops, SparseCore 0:
  93.7 85.9 all-gather.4
  181.4 105.5 all-gather.2

commit v4 on v3

--- a/solution.py
+++ b/solution.py
@@ -29,6 +29,10 @@
     else:
         g = lax.all_gather(factors, PAIR, axis=0, tiled=False)
         cube = g.transpose(1, 0, 2).reshape(nq, nvirt, nvirt)
+    return ladder_math(t, g, cube, nj, nvirt)
+
+
+def ladder_math(t, g, cube, nj, nvirt):
     parts = []
     for j in range(nj):
         tj = t[:, j].reshape(nvirt, nvirt)
@@ -63,7 +67,7 @@
     return out.reshape(nvirt, -1, nvirt)
 
 
-def on_device(amplitudes, factors, crossed_amplitudes, crossed_coupling):
+def on_device_body(amplitudes, factors, crossed_amplitudes, crossed_coupling):
     nvirt = NV
     norb = lax.axis_size("orb")
     nchip = lax.axis_size("zz")
@@ -93,7 +97,7 @@
     npair, norb = mesh.shape["pair"], mesh.shape["orb"]
     sub = Mesh(mesh.devices.reshape(npair // 2, 2, norb), ("zz", "core", "orb"))
     return jax.shard_map(
-        on_device,
+        on_device_body,
         mesh=sub,
         in_specs=(
             P(PAIR, None, "orb", None),

time: 502 us -> 498 us (level)
  starting transfers between devices: 25.1 us -> 37.4 us
  waiting for transfers between devices: 245 us -> 233 us
  matrix products: 137 us -> 129 us
    ppermute x3, waiting for transfers between devices: 73.9 us -> 61.4 us  [relay(): left = lax.ppermute(left, 'zz', [(j, j - 1) for j in range(1, n - s + 1)])]
    ppermute x3, starting transfers between devices: 10 us -> 22.4 us  [relay(): right = lax.ppermute(right, 'zz', [(i, i + 1) for i in range(s - 1, n - 1)])]
    dot_general x14, matrix products: 89.6 us -> 81.3 us  [crossed_term(): part = jnp.einsum('ak,nk->an', lhs, b, preferred_element_type=jnp.float32)]
  transfers between devices with their start and end apart: 19 -> 19, of which waited for: 6 -> 6; matrix products, arithmetic and copies ran while one was open for 28% -> 27% of each run, Pallas kernels for 0% -> 0%
where the time goes in v4:
time: 498 us; the launch traced here: 489 us
  waiting for transfers between devices  233 us (47%)
  matrix products  129 us (26%)
  local copies, waits for them, and re-layouts  70.3 us (14%)
  starting transfers between devices  37.4 us (8%)
  between operations  14.3 us (3%)
    dot_general x14, matrix products, crossed_term(): part = jnp.einsum('ak,nk->an', lhs, b, preferred_element_type=jnp.float32)  81.3 us
    all_gather x1, waiting for transfers between devices, ladder_term(): t = lax.all_gather(amplitudes[0], 'orb', axis=0, tiled=False)  78.4 us
    ppermute x3, waiting for transfers between devices, relay(): left = lax.ppermute(left, 'zz', [(j, j - 1) for j in range(1, n - s + 1)])  61.4 us
    ppermute x3, waiting for transfers between devices, relay(): right = lax.ppermute(right, 'zz', [(i, i + 1) for i in range(s - 1, n - 1)])  59.9 us
    ppermute x3, waiting for transfers between devices, reduce_scatter(): acc = acc + lax.ppermute(blk, 'orb', pairs)  32.7 us
    dot_general x2, matrix products, ladder_math(): jnp.einsum('pqad,rqbd->parb', inner, g, preferred_element_type=jnp.float32)  24.1 us
    dot_general x2, matrix products, ladder_math(): jnp.einsum('pqac,cd->pqad', g, tj, preferred_element_type=jnp.float32)  24 us
    ppermute x3, starting transfers between devices, relay(): right = lax.ppermute(right, 'zz', [(i, i + 1) for i in range(s - 1, n - 1)])  22.4 us
  transfers between devices with their start and end apart: 19, of which 6 were waited for; matrix products, arithmetic and copies ran while one was open for 27% of the time, Pallas kernels for 0%

profile of v4, /device:TPU:0, one launch (start us, length us, event | category | flops | bytes accessed | tf_op | source)
XLA Modules:
  0.0 488.8 jit_solution(11940839149197209218)
XLA Ops:
  6.5 10.4 %copy.22 = bf16[4,16,150,600]{3,1,2,0:T(8,128)(2,1)} copy(bf16[4,16,150,600]{3,1,0,2:T(8,128)(2,1)} %bitcast.156) | data formatting | bytes 23040000 | tf_op jit(solution)/shard_map/reshape;squeeze | solution.py:53
  17.0 6.5 %all-to-all-start = ((bf16[4,16,150,600]{3,1,2,0:T(8,128)(2,1)}), bf16[4,16,150,600]{3,1,2,0:T(8,128)(2,1)}, u32[]{:S(2)}, u32[]{:S(2)}) async-start(bf16[4,16,150,600]{3,1,2,0:T(8,128)(2,1)} %copy.22), calls=%async_computation | async-start | bytes 24576000 | tf_op jit(solution)/shard_map/all_to_all | solution.py:54
  23.5 6.6 %collective-permute-start.1 = (bf16[150,9600]{1,0:T(8,128)(2,1)}, bf16[150,9600]{1,0:T(8,128)(2,1)}, u32[]{:S(2)}, u32[]{:S(2)}) collective-permute-start(bf16[150,9600]{1,0:T(8,128)(2,1)} %bitcast.157), channel_id=1, source_target_pairs={{0,8},{8,16},{16,24},{1,9},{9,17},{17,25},{2,10},{10,18},{18,26},{... | collective-permute-start | bytes 8640008 | tf_op jit(solution)/shard_map/ppermute | solution.py:15
  30.1 1.3 collective-permute-start.3
  31.4 59.9 %collective-permute-done.1 = bf16[150,9600]{1,0:T(8,128)(2,1)} collective-permute-done((bf16[150,9600]{1,0:T(8,128)(2,1)}, bf16[150,9600]{1,0:T(8,128)(2,1)}, u32[]{:S(2)}, u32[]{:S(2)}) %collective-permute-start.1) | collective-permute-done | bytes 2880032 | tf_op jit(solution)/shard_map/ppermute | solution.py:15
  91.3 2.3 collective-permute-start.5
  93.8 3.2 collective-permute-done.3
  97.0 1.3 collective-permute-start.7
  98.3 3.0 all_gather_reshape.3
  101.3 78.4 %all-gather.5.cloned.1.call-done = bf16[4,2,150,600]{3,1,2,0:T(2,128)(2,1)} async-done(((bf16[1,2,150,600]{3,1,2,0:T(2,128)(2,1)}), bf16[4,2,150,600]{3,1,2,0:T(2,128)(2,1)}) %all-gather.5.cloned.1.call-update) | async-done | bytes 1440016 | tf_op jit(solution)/shard_map/all_gather | solution.py:24
  179.7 9.6 %slice_reduce_fusion.1 = (bf16[4,150,600]{2,1,0:T(8,128)(2,1)S(1)}, bf16[4,150,600]{2,1,0:T(8,128)(2,1)S(1)}) fusion(bf16[4,2,150,600]{3,1,2,0:T(2,128)(2,1)} %all-gather.5.cloned.1.call-done), kind=kLoop, calls=%fused_computation.14 | loop fusion | bytes 2880000 | tf_op jit(solution)/shard_map/slice | solution.py:38
  192.3 20.1 %reshape.12 = bf16[600,9600]{1,0:T(8,128)(2,1)} reshape(bf16[4,150,16,600]{3,2,1,0:T(8,128)(2,1)} %bitcast.12) | data formatting | bytes 23040000 | tf_op jit(solution)/shard_map/reshape | solution.py:55
  212.6 1.6 copy-done.5
  214.2 8.7 %fusion.22 = f32[600,8,150]{0,2,1:T(8,128)S(1)} fusion(f32[600,8,150]{0,2,1:T(8,128)S(1)} %broadcast_in_dim.48, s32[]{:T(128)S(6)} %select_n.68, bf16[600,9600]{1,0:T(8,128)(2,1)} %reshape.12, bf16[9600,150]{0,1:T(8,128)(2,1)S(1)} %copy-done.5), kind=kOutput, calls=%fused_computation.29 | convolution fusion | flops 1728000000 | bytes 14827524 | tf_op jit(solution)/shard_map/ak,nk->an/dot_general | solution.py:63
  222.9 13.5 %collective-permute-start.9 = (bf16[150,9600]{1,0:T(8,128)(2,1)}, bf16[150,9600]{1,0:T(8,128)(2,1)S(1)}, u32[]{:S(2)}, u32[]{:S(2)}) collective-permute-start(bf16[150,9600]{1,0:T(8,128)(2,1)} %collective-permute-done.5), channel_id=1, source_target_pairs={{16,24},{17,25},{18,26},{19,27},{20,28},{21,29},{22,30},{23,31}} | collective-permute-start | bytes 8640008 | tf_op jit(solution)/shard_map/ppermute | solution.py:15
  236.9 6.3 %fusion.24 = f32[600,8,150]{0,2,1:T(8,128)S(1)} fusion(f32[600,8,150]{0,2,1:T(8,128)S(1)} %fusion.22, s32[]{:T(128)S(6)} %select_n.69, bf16[600,9600]{1,0:T(8,128)(2,1)S(1)} %copy-done, bf16[150,9600]{1,0:T(8,128)(2,1)} %collective-permute-done), kind=kOutput, calls=%fused_computation.31 | convolution fusion | flops 1728089984 | bytes 15178244 | tf_op jit(solution)/shard_map/ak,nk->an/dot_general | solution.py:63
  243.1 6.3 %add_dynamic-update-slice_fusion.8 = f32[600,8,150]{0,2,1:T(8,128)S(1)} fusion(f32[600,8,150]{0,2,1:T(8,128)S(1)} %fusion.24, s32[]{:T(128)S(6)} %select_n.70, bf16[600,9600]{1,0:T(8,128)(2,1)S(1)} %copy-done, bf16[150,9600]{1,0:T(8,128)(2,1)} %collective-permute-done.1), kind=kOutput, calls=%fused_computation.55 | convolution fusion | flops 1728089984 | bytes 15178244 | tf_op jit(solution)/shard_map/ak,nk->an/dot_general | solution.py:63
  249.4 1.3 collective-permute-start.11
  250.7 6.2 %fusion.26 = f32[600,8,150]{0,2,1:T(8,128)S(1)} fusion(f32[600,8,150]{0,2,1:T(8,128)S(1)} %add_dynamic-update-slice_fusion.8, s32[]{:T(128)S(6)} %select_n.71, bf16[600,9600]{1,0:T(8,128)(2,1)S(1)} %copy-done, bf16[150,9600]{1,0:T(8,128)(2,1)} %collective-permute-done.2), kind=kOutput, calls=%fused_computation.33 | convolution fusion | flops 1728089984 | bytes 15178244 | tf_op jit(solution)/shard_map/ak,nk->an/dot_general | solution.py:63
  257.0 6.3 %add_dynamic-update-slice_fusion.7 = f32[600,8,150]{0,2,1:T(8,128)S(1)} fusion(f32[600,8,150]{0,2,1:T(8,128)S(1)} %fusion.26, s32[]{:T(128)S(6)} %select_n.72, bf16[600,9600]{1,0:T(8,128)(2,1)S(1)} %copy-done, bf16[150,9600]{1,0:T(8,128)(2,1)} %collective-permute-done.3), kind=kOutput, calls=%fused_computation.54 | convolution fusion | flops 1728089984 | bytes 15178244 | tf_op jit(solution)/shard_map/ak,nk->an/dot_general | solution.py:63
  263.3 6.2 %add_dynamic-update-slice_fusion.6 = f32[600,8,150]{0,2,1:T(8,128)S(1)} fusion(f32[600,8,150]{0,2,1:T(8,128)S(1)} %add_dynamic-update-slice_fusion.7, s32[]{:T(128)S(6)} %select_n.73, bf16[600,9600]{1,0:T(8,128)(2,1)S(1)} %copy-done, bf16[150,9600]{1,0:T(8,128)(2,1)} %collective-permute-done.4), kind=kOutput, calls=%fused_computation.53 | convolution fusion | flops 1728089984 | bytes 15178244 | tf_op jit(solution)/shard_map/ak,nk->an/dot_general | solution.py:63
  269.5 6.3 %add_dynamic-update-slice_fusion.5 = f32[600,8,150]{0,2,1:T(8,128)S(1)} fusion(f32[600,8,150]{0,2,1:T(8,128)S(1)} %add_dynamic-update-slice_fusion.6, s32[]{:T(128)S(6)} %select_n.74, bf16[600,9600]{1,0:T(8,128)(2,1)S(1)} %copy-done, bf16[150,9600]{1,0:T(8,128)(2,1)} %collective-permute-done.5), kind=kOutput, calls=%fused_computation.52 | convolution fusion | flops 1728089984 | bytes 15178244 | tf_op jit(solution)/shard_map/ak,nk->an/dot_general | solution.py:63
  275.9 58.2 %collective-permute-done.11 = bf16[150,9600]{1,0:T(8,128)(2,1)S(1)} collective-permute-done((bf16[150,9600]{1,0:T(8,128)(2,1)}, bf16[150,9600]{1,0:T(8,128)(2,1)S(1)}, u32[]{:S(2)}, u32[]{:S(2)}) %collective-permute-start.11) | collective-permute-done | bytes 2880032 | tf_op jit(solution)/shard_map/ppermute | solution.py:16
  334.1 6.6 %fusion.28 = f32[600,8,150]{0,2,1:T(8,128)S(1)} fusion(f32[600,8,150]{0,2,1:T(8,128)S(1)} %add_dynamic-update-slice_fusion.5, s32[]{:T(128)S(6)} %select_n.75, bf16[600,9600]{1,0:T(8,128)(2,1)S(1)} %copy-done, bf16[150,9600]{1,0:T(8,128)(2,1)} %collective-permute-done.6), kind=kOutput, calls=%fused_computation.35 | convolution fusion | flops 1728089984 | bytes 15178244 | tf_op jit(solution)/shard_map/ak,nk->an/dot_general | solution.py:63
  340.8 6.2 %add_dynamic-update-slice_fusion.4 = f32[600,8,150]{0,2,1:T(8,128)S(1)} fusion(f32[600,8,150]{0,2,1:T(8,128)S(1)} %fusion.28, s32[]{:T(128)S(6)} %select_n.76, bf16[600,9600]{1,0:T(8,128)(2,1)S(1)} %copy-done, bf16[150,9600]{1,0:T(8,128)(2,1)} %collective-permute-done.7), kind=kOutput, calls=%fused_computation.51 | convolution fusion | flops 1728089984 | bytes 15178244 | tf_op jit(solution)/shard_map/ak,nk->an/dot_general | solution.py:63
  347.0 4.4 add_dynamic-update-slice_fusion.3
  351.4 4.4 add_dynamic-update-slice_fusion.2
  355.8 4.6 fusion.30
  360.4 4.4 add_dynamic-update-slice_fusion.1
  364.8 4.4 add_dynamic-update-slice_fusion
  369.2 5.3 %reshape.23 = f32[4,150,2,600]{1,0,3,2:T(4,128)} reshape(f32[600,8,150]{0,2,1:T(8,128)S(1)} %add_dynamic-update-slice_fusion) | data formatting | bytes 5760000 | tf_op jit(solution)/shard_map/reshape | solution.py:67
  374.5 6.2 %copy.24 = f32[4,150,2,600]{3,1,0,2:T(8,128)} copy(f32[4,150,2,600]{1,0,3,2:T(4,128)} %reshape.23) | data formatting | bytes 5760000 | tf_op jit(solution)/shard_map/reshape | solution.py:67
  380.8 12.5 %fusion.77 = bf16[8,12,75,600,1]{3,2,1,4,0:T(8,128)(2,1)S(1)} fusion(bf16[8,12,75,600]{3,2,1,0:T(8,128)(2,1)} %all-gather.3.cloned.1.call-done, bf16[600,600,1,1]{1,0,2,3:T(8,128)(2,1)S(1)} %copy-done.3), kind=kOutput, calls=%fused_computation.3.clone.clone.clone.1 | convolution fusion | flops 5188320256 | bytes 18000000 | tf_op jit(solution)/shard_map/pqac,cd->pqad/dot_general | solution.py:40
  393.3 10.8 %fusion.12 = f32[8,75,8,75]{3,1,2,0:T(8,128)S(1)} fusion(bf16[8,12,75,600]{3,2,1,0:T(8,128)(2,1)S(1)} %copy-done.4, bf16[8,12,75,600,1]{3,2,1,4,0:T(8,128)(2,1)S(1)} %fusion.77), kind=kOutput, calls=%fused_computation.11 | convolution fusion | flops 5184000000 | bytes 18720000 | tf_op jit(solution)/shard_map/pqad,rqbd->parb/dot_general | solution.py:41
  404.9 2.3 stack.7
  407.2 11.5 %fusion.81 = bf16[8,12,75,600,1]{3,2,1,4,0:T(8,128)(2,1)S(1)} fusion(bf16[8,12,75,600]{3,2,1,0:T(8,128)(2,1)} %all-gather.3.cloned.1.call-done, bf16[600,600,1,1]{1,0,2,3:T(8,128)(2,1)S(1)} %copy-done.2), kind=kOutput, calls=%fused_computation.1.clone.clone.clone | convolution fusion | flops 5188320256 | bytes 18000000 | tf_op jit(solution)/shard_map/pqac,cd->pqad/dot_general | solution.py:40
  418.7 13.2 %fusion.17 = f32[8,75,8,75]{3,1,2,0:T(8,128)S(1)} fusion(bf16[8,12,75,600]{3,2,1,0:T(8,128)(2,1)} %all-gather.3.cloned.1.call-done, bf16[8,12,75,600,1]{3,2,1,4,0:T(8,128)(2,1)S(1)} %fusion.81), kind=kOutput, calls=%fused_computation.12 | convolution fusion | flops 5184000000 | bytes 18720000 | tf_op jit(solution)/shard_map/pqad,rqbd->parb/dot_general | solution.py:41
  432.7 2.4 stack.8
  435.0 3.1 maximum_add_fusion
  438.3 1.3 copy.25
  439.6 1.5 collective-permute-start.13
  441.1 1.3 copy.27
  442.4 1.5 collective-permute-start.14
  443.9 1.3 copy.29
  445.7 14.3 %collective-permute-done.13 = f32[150,2,600]{2,1,0:T(2,128)} collective-permute-done((f32[150,2,600]{2,1,0:T(2,128)}, f32[150,2,600]{2,1,0:T(2,128)}, u32[]{:S(2)}, u32[]{:S(2)}) %collective-permute-start.13) | collective-permute-done | bytes 720032 | tf_op jit(solution)/shard_map/ppermute | solution.py:92
  460.0 18.4 %collective-permute-done.14 = f32[150,2,600]{2,1,0:T(2,128)} collective-permute-done((f32[150,2,600]{2,1,0:T(2,128)}, f32[150,2,600]{2,1,0:T(2,128)}, u32[]{:S(2)}, u32[]{:S(2)}) %collective-permute-start.14) | collective-permute-done | bytes 720032 | tf_op jit(solution)/shard_map/ppermute | solution.py:92
  478.4 1.8 fusion.33
  480.2 1.3 copy.31
  (42 shorter events, 6.1 us)
Async XLA Ops:
  17.0 81.3 %copy-start.1 = (bf16[12,45000]{1,0:T(8,128)(2,1)S(1)}, bf16[12,45000]{1,0:T(8,128)(2,1)}, u32[]{:S(2)}) copy-start(bf16[12,45000]{1,0:T(8,128)(2,1)} %param.5) | copy-start | bytes 3240004
  17.0 175.4 %all-to-all-start = ((bf16[4,16,150,600]{3,1,2,0:T(8,128)(2,1)}), bf16[4,16,150,600]{3,1,2,0:T(8,128)(2,1)}, u32[]{:S(2)}, u32[]{:S(2)}) async-start(bf16[4,16,150,600]{3,1,2,0:T(8,128)(2,1)} %copy.22), calls=%async_computation | async-start | bytes 24576000 | tf_op jit(solution)/shard_map/all_to_all | solution.py:54
  23.5 156.3 %all-gather.5.cloned.1.call-start = ((), (), s32[]{:S(2)}) async-start(), calls=%async_computation.2 | async-start | bytes 1920000 | tf_op jit(solution)/shard_map/all_gather | solution.py:24
  23.5 67.8 %collective-permute-start.1 = (bf16[150,9600]{1,0:T(8,128)(2,1)}, bf16[150,9600]{1,0:T(8,128)(2,1)}, u32[]{:S(2)}, u32[]{:S(2)}) collective-permute-start(bf16[150,9600]{1,0:T(8,128)(2,1)} %bitcast.157), channel_id=1, source_target_pairs={{0,8},{8,16},{16,24},{1,9},{9,17},{17,25},{2,10},{10,18},{18,26},{... | collective-permute-start | bytes 8640008 | tf_op jit(solution)/shard_map/ppermute | solution.py:15
  30.1 66.9 %collective-permute-start.3 = (bf16[150,9600]{1,0:T(8,128)(2,1)}, bf16[150,9600]{1,0:T(8,128)(2,1)}, u32[]{:S(2)}, u32[]{:S(2)}) collective-permute-start(bf16[150,9600]{1,0:T(8,128)(2,1)} %bitcast.158), channel_id=1, source_target_pairs={{8,0},{16,8},{24,16},{9,1},{17,9},{25,17},{10,2},{18,10},{26,18},{... | collective-permute-start | bytes 8640008 | tf_op jit(solution)/shard_map/ppermute | solution.py:16
  91.3 101.1 %collective-permute-start.5 = (bf16[150,9600]{1,0:T(8,128)(2,1)}, bf16[150,9600]{1,0:T(8,128)(2,1)}, u32[]{:S(2)}, u32[]{:S(2)}) collective-permute-start(bf16[150,9600]{1,0:T(8,128)(2,1)} %collective-permute-done.1), channel_id=1, source_target_pairs={{8,16},{16,24},{9,17},{17,25},{10,18},{18,26},{11,19},{19,27},{12,... | collective-permute-start | bytes 8640008 | tf_op jit(solution)/shard_map/ppermute | solution.py:15
  93.6 287.2 %all-gather.3.cloned.1.call-start = ((), (), s32[]{:S(2)}) async-start(), calls=%async_computation.1 | async-start | bytes 11059200 | tf_op jit(solution)/shard_map/all_gather | solution.py:27
  93.7 129.2 %collective-permute-start = (bf16[150,9600]{1,0:T(8,128)(2,1)}, bf16[150,9600]{1,0:T(8,128)(2,1)}, u32[]{:S(2)}, u32[]{:S(2)}) collective-permute-start(bf16[150,9600]{1,0:T(8,128)(2,1)} %bitcast.159), channel_id=1, source_target_pairs={{0,4},{4,0},{1,5},{5,1},{2,6},{6,2},{3,7},{7,3},{8,12},{12,8},{9,1... | collective-permute-start | bytes 8640008 | tf_op jit(solution)/shard_map/ppermute | solution.py:61
  97.0 139.4 %collective-permute-start.7 = (bf16[150,9600]{1,0:T(8,128)(2,1)}, bf16[150,9600]{1,0:T(8,128)(2,1)}, u32[]{:S(2)}, u32[]{:S(2)}) collective-permute-start(bf16[150,9600]{1,0:T(8,128)(2,1)} %collective-permute-done.3), channel_id=1, source_target_pairs={{8,0},{16,8},{9,1},{17,9},{10,2},{18,10},{11,3},{19,11},{12,4},{20... | collective-permute-start | bytes 8640008 | tf_op jit(solution)/shard_map/ppermute | solution.py:16
  191.8 57.6 %collective-permute-start.2 = (bf16[150,9600]{1,0:T(8,128)(2,1)}, bf16[150,9600]{1,0:T(8,128)(2,1)}, u32[]{:S(2)}, u32[]{:S(2)}) collective-permute-start(bf16[150,9600]{1,0:T(8,128)(2,1)} %collective-permute-done.1), channel_id=1, source_target_pairs={{0,4},{4,0},{1,5},{5,1},{2,6},{6,2},{3,7},{7,3},{8,12},{12,8},{9,1... | collective-permute-start | bytes 8640008 | tf_op jit(solution)/shard_map/ppermute | solution.py:61
  191.8 71.5 %collective-permute-start.4 = (bf16[150,9600]{1,0:T(8,128)(2,1)}, bf16[150,9600]{1,0:T(8,128)(2,1)}, u32[]{:S(2)}, u32[]{:S(2)}) collective-permute-start(bf16[150,9600]{1,0:T(8,128)(2,1)} %collective-permute-done.3), channel_id=1, source_target_pairs={{0,4},{4,0},{1,5},{5,1},{2,6},{6,2},{3,7},{7,3},{8,12},{12,8},{9,1... | collective-permute-start | bytes 8640008 | tf_op jit(solution)/shard_map/ppermute | solution.py:61
  192.3 141.8 %collective-permute-start.6 = (bf16[150,9600]{1,0:T(8,128)(2,1)}, bf16[150,9600]{1,0:T(8,128)(2,1)}, u32[]{:S(2)}, u32[]{:S(2)}) collective-permute-start(bf16[150,9600]{1,0:T(8,128)(2,1)} %collective-permute-done.5), channel_id=1, source_target_pairs={{0,4},{4,0},{1,5},{5,1},{2,6},{6,2},{3,7},{7,3},{8,12},{12,8},{9,1... | collective-permute-start | bytes 8640008 | tf_op jit(solution)/shard_map/ppermute | solution.py:61
  212.4 1.8 copy-start.5
  214.2 22.6 %copy-start = (bf16[600,9600]{1,0:T(8,128)(2,1)S(1)}, bf16[600,9600]{1,0:T(8,128)(2,1)}, u32[]{:S(2)}) copy-start(bf16[600,9600]{1,0:T(8,128)(2,1)} %reshape.12) | copy-start | bytes 34560004
  222.9 52.9 %collective-permute-start.9 = (bf16[150,9600]{1,0:T(8,128)(2,1)}, bf16[150,9600]{1,0:T(8,128)(2,1)S(1)}, u32[]{:S(2)}, u32[]{:S(2)}) collective-permute-start(bf16[150,9600]{1,0:T(8,128)(2,1)} %collective-permute-done.5), channel_id=1, source_target_pairs={{16,24},{17,25},{18,26},{19,27},{20,28},{21,29},{22,30},{23,31}} | collective-permute-start | bytes 8640008 | tf_op jit(solution)/shard_map/ppermute | solution.py:15
  236.4 110.6 %collective-permute-start.8 = (bf16[150,9600]{1,0:T(8,128)(2,1)}, bf16[150,9600]{1,0:T(8,128)(2,1)S(1)}, u32[]{:S(2)}, u32[]{:S(2)}) collective-permute-start(bf16[150,9600]{1,0:T(8,128)(2,1)} %collective-permute-done.7), channel_id=1, source_target_pairs={{0,4},{4,0},{1,5},{5,1},{2,6},{6,2},{3,7},{7,3},{8,12},{12,8},{9,1... | collective-permute-start | bytes 8640008 | tf_op jit(solution)/shard_map/ppermute | solution.py:61
  249.4 84.7 %collective-permute-start.11 = (bf16[150,9600]{1,0:T(8,128)(2,1)}, bf16[150,9600]{1,0:T(8,128)(2,1)S(1)}, u32[]{:S(2)}, u32[]{:S(2)}) collective-permute-start(bf16[150,9600]{1,0:T(8,128)(2,1)} %collective-permute-done.7), channel_id=1, source_target_pairs={{8,0},{9,1},{10,2},{11,3},{12,4},{13,5},{14,6},{15,7}} | collective-permute-start | bytes 8640008 | tf_op jit(solution)/shard_map/ppermute | solution.py:16
  275.9 80.0 %collective-permute-start.10 = (bf16[150,9600]{1,0:T(8,128)(2,1)S(1)}, bf16[150,9600]{1,0:T(8,128)(2,1)S(1)}, u32[]{:S(2)}, u32[]{:S(2)}) collective-permute-start(bf16[150,9600]{1,0:T(8,128)(2,1)S(1)} %collective-permute-done.9), channel_id=1, source_target_pairs={{0,4},{4,0},{1,5},{5,1},{2,6},{6,2},{3,7},{7,3},{8,12},{12,8},{9,1... | collective-permute-start | bytes 8640008 | tf_op jit(solution)/shard_map/ppermute | solution.py:61
  334.1 30.7 %collective-permute-start.12 = (bf16[150,9600]{1,0:T(8,128)(2,1)S(1)}, bf16[150,9600]{1,0:T(8,128)(2,1)S(1)}, u32[]{:S(2)}, u32[]{:S(2)}) collective-permute-start(bf16[150,9600]{1,0:T(8,128)(2,1)S(1)} %collective-permute-done.11), channel_id=1, source_target_pairs={{0,4},{4,0},{1,5},{5,1},{2,6},{6,2},{3,7},{7,3},{8,12},{12,8},{9,1... | collective-permute-start | bytes 8640008 | tf_op jit(solution)/shard_map/ppermute | solution.py:61
  374.5 6.2 %copy-start.3 = (bf16[600,600,1,1]{1,0,2,3:T(8,128)(2,1)S(1)}, bf16[600,600,1,1]{1,0,2,3:T(8,128)(2,1)}, u32[]{:S(2)}) copy-start(bf16[600,600,1,1]{1,0,2,3:T(8,128)(2,1)} %reshape.14) | copy-start | bytes 2160004
  380.8 12.5 %copy-start.4 = (bf16[8,12,75,600]{3,2,1,0:T(8,128)(2,1)S(1)}, bf16[8,12,75,600]{3,2,1,0:T(8,128)(2,1)}, u32[]{:S(2)}) copy-start(bf16[8,12,75,600]{3,2,1,0:T(8,128)(2,1)} %all-gather.3.cloned.1.call-done) | copy-start | bytes 25920004
  404.9 2.3 copy-start.2
  439.6 20.3 %collective-permute-start.13 = (f32[150,2,600]{2,1,0:T(2,128)}, f32[150,2,600]{2,1,0:T(2,128)}, u32[]{:S(2)}, u32[]{:S(2)}) collective-permute-start(f32[150,2,600]{2,1,0:T(2,128)} %copy.25), channel_id=1, source_target_pairs={{0,1},{1,0},{2,3},{3,2},{4,5},{5,4},{6,7},{7,6},{8,9},{9,8},{10,11... | collective-permute-start | bytes 2160008 | tf_op jit(solution)/shard_map/ppermute | solution.py:92
  442.4 36.0 %collective-permute-start.14 = (f32[150,2,600]{2,1,0:T(2,128)}, f32[150,2,600]{2,1,0:T(2,128)}, u32[]{:S(2)}, u32[]{:S(2)}) collective-permute-start(f32[150,2,600]{2,1,0:T(2,128)} %copy.27), channel_id=1, source_target_pairs={{0,2},{1,3},{2,0},{3,1},{4,6},{5,7},{6,4},{7,5},{8,10},{9,11},{10,... | collective-permute-start | bytes 2160008 | tf_op jit(solution)/shard_map/ppermute | solution.py:92
  445.2 33.2 %collective-permute-start.15 = (f32[150,2,600]{2,1,0:T(2,128)}, f32[150,2,600]{2,1,0:T(2,128)}, u32[]{:S(2)}, u32[]{:S(2)}) collective-permute-start(f32[150,2,600]{2,1,0:T(2,128)} %copy.29), channel_id=1, source_target_pairs={{0,3},{1,2},{2,1},{3,0},{4,7},{5,6},{6,5},{7,4},{8,11},{9,10},{10,... | collective-permute-start | bytes 2160008 | tf_op jit(solution)/shard_map/ppermute | solution.py:92
Sparse Core Ops, SparseCore 0:
  93.7 85.9 all-gather.4
  181.4 100.0 all-gather.2
